TPU v7x, 512 devices: a whole 4x8x8 slice. The times are simulated.
512 devices in a mesh: fsdp: 128 (over z, y, core), tp: 4 (over x).
Axes of the slice: x: 4, y: 8, z: 8, core: 2. Of those that a mesh axis runs over, the one named last changes fastest.
Arguments:
- q_grad: bfloat16 [128, 1280, 768], P('fsdp', None, 'tp'), may hold values from -24 to 24, as said below
- o_grad: bfloat16 [128, 768, 1280], P('fsdp', 'tp'), may hold values from -24 to 24, as said below
- norm_grad: float32 [128, 4, 1344], P('fsdp', 'tp'), may hold values from -6 to 6, as said below
- emb_grad: bfloat16 [8192, 1280], P('fsdp', 'tp'), may hold values from -6 to 6, as said below
- flat_master: float32 [4, 491520], P('tp', 'fsdp'), may hold values from -0.15625 to 0.15625
- flat_first: float32 [4, 491520], P('tp', 'fsdp'), may hold values from -0.75 to 0.75
- flat_second: float32 [4, 491520], P('tp', 'fsdp'), may hold values from 0.001 to 0.1
- emb_master: float32 [8192, 1280], P(('fsdp', 'tp')), may hold values from -0.3125 to 0.3125
- emb_first: float32 [8192, 1280], P(('fsdp', 'tp')), may hold values from -0.75 to 0.75
- emb_second: float32 [8192, 1280], P(('fsdp', 'tp')), may hold values from 0.001 to 0.1
- norm_master: float32 [1344], replicated, may hold values from 0.5 to 1.5
- norm_first: float32 [1344], replicated, may hold values from -0.75 to 0.75
- norm_second: float32 [1344], replicated, may hold values from 0.001 to 0.1
- step_count: int32 [1], replicated, may hold values from 1 to 64
Outputs:
- new_flat_master: float32 [4, 491520], P('tp', 'fsdp')
- new_flat_first: float32 [4, 491520], P('tp', 'fsdp')
- new_flat_second: float32 [4, 491520], P('tp', 'fsdp')
- new_emb_master: float32 [8192, 1280], P(('fsdp', 'tp'))
- new_emb_first: float32 [8192, 1280], P(('fsdp', 'tp'))
- new_emb_second: float32 [8192, 1280], P(('fsdp', 'tp'))
- new_norm_master: float32 [1344], replicated
- new_norm_first: float32 [1344], replicated
- new_norm_second: float32 [1344], replicated
- q_weight: bfloat16 [1280, 768], P(None, 'tp')
- o_weight: bfloat16 [768, 1280], P('tp')
- q_average: bfloat16 [1280, 768], P('fsdp')
- o_average: bfloat16 [768, 1280], P(None, 'fsdp')
- emb_weight: bfloat16 [8192, 1280], P('fsdp', 'tp')
Inputs may be any that keep to these rules, and one draw needn't show every extreme that they name: `q_grad`: each data replica's gradient of the query projection. `o_grad`: each data replica's gradient of the output projection. `norm_grad`: each device's gradient of the gains. `emb_grad`: the embedding slice's summed gradient.
All inputs are finite; a program needn't handle non-finite values.
Results may differ from a plain program's by a relative error of at most 0.0004.
Values may be sent and summed in bfloat16 or wider, within the bound.
No kernel may reach another device: no remote copies, remote signals or barrier semaphores. Data moves between devices by JAX's collectives and lax.ppermute only.
A program may use at most 64 MiB of HBM per device.

v0:
```python
import math

import jax
import jax.numpy as jnp
from jax import lax
from jax.sharding import PartitionSpec as P

BETA_ONE = 0.9
BETA_TWO = 0.95
EPSILON = 1e-08
LEARN_RATE = 0.0053


def adam_update(weights_in, first_in, second_in, gradient, first_fix, second_fix, decay_rate):
    first_out = BETA_ONE * first_in + (1.0 - BETA_ONE) * gradient
    second_out = BETA_TWO * second_in + (1.0 - BETA_TWO) * gradient * gradient
    update = first_out / first_fix / (jnp.sqrt(second_out / second_fix) + EPSILON)
    weights_out = weights_in - LEARN_RATE * (update + decay_rate * weights_in)
    return (weights_out, first_out, second_out)


def body(
    q_grad,
    o_grad,
    norm_grad,
    emb_grad,
    flat_master,
    flat_first,
    flat_second,
    emb_master,
    emb_first,
    emb_second,
    norm_master,
    norm_first,
    norm_second,
    step_count,
):
    fsdp_count = lax.axis_size("fsdp")
    tp_count = lax.axis_size("tp")
    width = q_grad.shape[1]
    q_columns = q_grad.shape[2]
    entry_count = (
        2 * width * q_columns * tp_count
        + emb_grad.shape[0] * fsdp_count * width
        + norm_master.shape[0]
    )
    clip_limit = 0.5 * math.sqrt(entry_count)
    local_flat = jnp.concatenate([q_grad[0].reshape(-1), o_grad[0].reshape(-1)])
    piece_len = local_flat.shape[0] // fsdp_count
    summed = lax.psum(local_flat.astype(jnp.float32), "fsdp")
    grad_piece = lax.dynamic_slice_in_dim(summed, lax.axis_index("fsdp") * piece_len, piece_len, 0)
    emb_piece = lax.all_to_all(emb_grad, "tp", split_axis=0, concat_axis=1, tiled=True).astype(
        jnp.float32
    )
    local_squares = jnp.sum(grad_piece * grad_piece) + jnp.sum(emb_piece * emb_piece)
    gains_local = norm_grad[0, 0]
    gain_sum = lax.psum(gains_local, ("fsdp", "tp"))
    global_squares = lax.psum(local_squares, ("fsdp", "tp"))
    grad_norm = jnp.sqrt(global_squares + jnp.sum(gain_sum * gain_sum))
    clip_factor = jnp.minimum(jnp.float32(1.0), clip_limit / (grad_norm + 1e-06))
    step_value = step_count[0].astype(jnp.float32)
    first_fix = 1.0 - jnp.power(jnp.float32(BETA_ONE), step_value)
    second_fix = 1.0 - jnp.power(jnp.float32(BETA_TWO), step_value)
    flat_new, flat_one, flat_two = adam_update(
        flat_master[0],
        flat_first[0],
        flat_second[0],
        clip_factor * grad_piece,
        first_fix,
        second_fix,
        0.1,
    )
    emb_new, emb_one, emb_two = adam_update(
        emb_master, emb_first, emb_second, clip_factor * emb_piece, first_fix, second_fix, 0.1
    )
    norm_new, norm_one, norm_two = adam_update(
        norm_master, norm_first, norm_second, clip_factor * gain_sum, first_fix, second_fix, 0.0
    )
    gathered = lax.all_gather(flat_new.astype(jnp.bfloat16), "fsdp", axis=0, tiled=True)
    q_weight = gathered[: width * q_columns].reshape(width, q_columns)
    o_weight = gathered[width * q_columns :].reshape(q_columns, width)
    block_rows = width // fsdp_count
    block_start = lax.axis_index("fsdp") * block_rows
    q_block = lax.dynamic_slice_in_dim(q_weight, block_start, block_rows, 0)
    o_block = lax.dynamic_slice_in_dim(o_weight, block_start, block_rows, 1)
    q_average, o_average = (
        lax.all_gather(q_block, "tp", axis=1, tiled=True),
        lax.all_gather(o_block, "tp", axis=0, tiled=True),
    )
    emb_weight = lax.all_to_all(
        emb_new.astype(jnp.bfloat16), "tp", split_axis=1, concat_axis=0, tiled=True
    )
    return (
        flat_new[None, :],
        flat_one[None, :],
        flat_two[None, :],
        emb_new,
        emb_one,
        emb_two,
        norm_new,
        norm_one,
        norm_two,
        q_weight,
        o_weight,
        q_average,
        o_average,
        emb_weight,
    )


def solution(mesh):
    return jax.shard_map(
        body,
        mesh=mesh,
        in_specs=(
            P("fsdp", None, "tp"),
            P("fsdp", "tp", None),
            P("fsdp", "tp", None),
            P("fsdp", "tp"),
            P("tp", "fsdp"),
            P("tp", "fsdp"),
            P("tp", "fsdp"),
            P(("fsdp", "tp"), None),
            P(("fsdp", "tp"), None),
            P(("fsdp", "tp"), None),
            P(),
            P(),
            P(),
            P(),
        ),
        out_specs=(
            P("tp", "fsdp"),
            P("tp", "fsdp"),
            P("tp", "fsdp"),
            P(("fsdp", "tp"), None),
            P(("fsdp", "tp"), None),
            P(("fsdp", "tp"), None),
            P(),
            P(),
            P(),
            P(None, "tp"),
            P("tp", None),
            P("fsdp", None),
            P(None, "fsdp"),
            P("fsdp", "tp"),
        ),
        check_vma=False,
    )
```

profile of v0, /device:TPU:26, one launch (start us, length us, event | category | flops | bytes accessed | tf_op | source)
XLA Modules:
  0.0 419.5 jit_solution(9161934839932907746)
XLA Ops:
  7.2 0.0 copy-start.1
  7.2 0.0 all-reduce.3.cloned.1.call-start
  7.2 1.3 copy.56
  8.6 0.8 reshape_squeeze.6
  9.3 0.0 copy-done.1
  9.3 0.6 reshape_squeeze.7
  9.9 0.0 copy-start.6
  9.9 0.0 copy-start.7
  10.0 0.0 copy-start.11
  10.0 0.0 copy-start.5
  10.0 1.4 maximum_convert_fusion
  11.4 0.0 all-reduce.3.cloned.1.call-update
  11.4 4.8 %all-to-all-start = ((bf16[4,16,320]{2,1,0:T(8,128)(2,1)}), bf16[4,16,320]{2,1,0:T(8,128)(2,1)S(1)}, u32[]{:S(2)}, u32[]{:S(2)}) async-start(bf16[4,16,320]{2,1,0:T(8,128)(2,1)} %bitcast), calls=%async_computation | async-start | bytes 98304 | tf_op jit(solution)/shard_map/all_to_all | solution.py:52
  16.3 0.0 copy-done.6
  16.3 0.0 copy-done.7
  16.3 0.1 multiply_reduce_fusion.1
  17.1 0.0 copy-done.11
  17.1 0.0 copy-done.5
  17.2 3.1 all-to-all-done
  20.3 0.6 fusion
  21.0 198.5 %all-reduce.3.cloned.1.call-done = f32[491520]{0:T(1024)} async-done(((f32[491520]{0:T(1024)}), f32[491520]{0:T(1024)}) %all-reduce.3.cloned.1.call-update) | async-done | bytes 1966096 | tf_op jit(solution)/shard_map/psum | solution.py:50
  219.5 1.4 multiply_reduce_fusion
  222.2 95.3 %all-reduce = (f32[]{:T(128)}, f32[1344]{0:T(1024)S(1)}) all-reduce(f32[]{:T(128)S(6)} %add.68, f32[1344]{0:T(1024)S(1)} %reduce.4), channel_id=1, replica_groups=mesh['fsdp'=128,'tp'=4] {'fsdp','tp'}, use_global_device_ids=true, to_apply=%region_3.0 | all-reduce | flops 1345 | bytes 10760 | tf_op jit(solution)/shard_map/psum | solution.py:58
  317.5 0.6 multiply_reduce_fusion.3
  319.5 0.8 fusion.7
  320.3 51.2 %all-gather = bf16[128,1,3840]{2,1,0:T(2,128)(2,1)S(1)} all-gather(bf16[1,1,3840]{2,1,0:T(2,128)(2,1)S(1)} %reshape.68), channel_id=1, replica_groups=mesh['fsdp'=128,'tp'=4] {'fsdp'}, dimensions={0}, use_global_device_ids=true | all-gather | bytes 990720 | tf_op jit(solution)/shard_map/all_gather | solution.py:79
  371.5 4.3 %slice_reduce_fusion = (bf16[64,3840]{1,0:T(8,128)(2,1)S(1)}, bf16[64,3840]{1,0:T(8,128)(2,1)S(1)}) fusion(bf16[128,1,3840]{2,1,0:T(2,128)(2,1)S(1)} %all-gather), kind=kLoop, calls=%fused_computation | loop fusion | bytes 1966080 | tf_op jit(solution)/shard_map/slice | solution.py:81
  375.8 0.0 copy-start.2
  375.8 0.0 copy-start.3
  375.8 0.0 copy-start.4
  375.8 0.0 copy-start.8
  375.8 0.0 copy-start.9
  375.9 0.0 copy-start.10
  375.9 0.8 slice.27
  376.7 0.2 slice.29
  376.9 0.0 copy-start
  377.0 0.1 mul.176
  377.1 0.0 copy-done.2
  377.1 0.0 copy-done.3
  377.1 0.0 copy-done.4
  377.1 0.7 fusion.5
  377.9 0.1 all_to_all.26
  378.0 0.6 copy.61
  378.6 4.4 %all-to-all-start.1 = ((bf16[16,4,320]{2,0,1:T(8,128)(2,1)}), bf16[16,4,320]{2,0,1:T(8,128)(2,1)S(1)}, u32[]{:S(2)}, u32[]{:S(2)}) async-start(bf16[16,4,320]{2,0,1:T(8,128)(2,1)} %copy.61), calls=%async_computation.1 | async-start | bytes 98304 | tf_op jit(solution)/shard_map/all_to_all | solution.py:90
  383.0 0.1 constant_dynamic-slice_fusion
  383.1 0.0 copy-done.8
  383.1 0.0 copy-done.9
  383.1 0.0 copy-done.10
  383.2 0.6 multiply_subtract_fusion.2
  383.8 1.0 copy.62
  384.8 11.9 %all-gather.1 = bf16[4,192,10]{1,2,0:T(8,128)(2,1)S(1)} all-gather(bf16[1,192,10]{1,2,0:T(8,128)(2,1)S(1)} %dynamic-slice_bitcast_fusion), channel_id=1, replica_groups=mesh['fsdp'=128,'tp'=4] {'tp'}, dimensions={0}, use_global_device_ids=true | all-gather | bytes 19200 | tf_op jit(solution)/shard_map/all_gather | solution.py:87
  396.7 0.7 reshape.71
  397.4 0.1 copy.59
  397.5 11.9 %all-gather.2 = bf16[4,192,10]{1,2,0:T(8,128)(2,1)S(1)} all-gather(bf16[1,192,10]{1,2,0:T(8,128)(2,1)S(1)} %bitcast.19), channel_id=1, replica_groups=mesh['fsdp'=128,'tp'=4] {'tp'}, dimensions={0}, use_global_device_ids=true | all-gather | bytes 19200 | tf_op jit(solution)/shard_map/all_gather | solution.py:88
  409.5 0.7 reshape.73
  410.2 0.6 broadcast_in_dim.10
  410.8 0.6 broadcast_in_dim.11
  411.4 0.6 broadcast_in_dim.9
  412.0 0.0 all-to-all-done.1
  412.0 0.6 copy.66
  412.6 0.0 copy-done
  (8 shorter events, 0.2 us)
Async XLA Ops:
  7.2 2.2 copy-start.1
  7.2 212.3 %all-reduce.3.cloned.1.call-start = ((), (), s32[]{:S(2)}) async-start(), calls=%async_computation.2 | async-start | bytes 3932160 | tf_op jit(solution)/shard_map/psum | solution.py:50
  9.9 6.3 %copy-start.6 = (f32[1,3840]{1,0:T(1,128)S(1)}, f32[1,3840]{1,0:T(1,128)}, u32[]{:S(2)}) copy-start(f32[1,3840]{1,0:T(1,128)} %param.20) | copy-start | bytes 46084
  9.9 6.3 %copy-start.7 = (f32[1,3840]{1,0:T(1,128)S(1)}, f32[1,3840]{1,0:T(1,128)}, u32[]{:S(2)}) copy-start(f32[1,3840]{1,0:T(1,128)} %param.19) | copy-start | bytes 46084
  10.0 7.1 %copy-start.11 = (f32[1,1,1344]{2,1,0:T(1,128)S(1)}, f32[1,1,1344]{2,1,0:T(1,128)}, u32[]{:S(2)}) copy-start(f32[1,1,1344]{2,1,0:T(1,128)} %param.16) | copy-start | bytes 16132
  10.0 7.2 %copy-start.5 = (f32[1,3840]{1,0:T(1,128)S(1)}, f32[1,3840]{1,0:T(1,128)}, u32[]{:S(2)}) copy-start(f32[1,3840]{1,0:T(1,128)} %param.18) | copy-start | bytes 46084
  11.4 8.9 %all-to-all-start = ((bf16[4,16,320]{2,1,0:T(8,128)(2,1)}), bf16[4,16,320]{2,1,0:T(8,128)(2,1)S(1)}, u32[]{:S(2)}, u32[]{:S(2)}) async-start(bf16[4,16,320]{2,1,0:T(8,128)(2,1)} %bitcast), calls=%async_computation | async-start | bytes 98304 | tf_op jit(solution)/shard_map/all_to_all | solution.py:52
  375.8 1.3 copy-start.2
  375.8 1.3 copy-start.3
  375.8 1.3 copy-start.4
  375.8 7.3 %copy-start.8 = (f32[1344]{0:T(1024)S(1)}, f32[1344]{0:T(1024)}, u32[]{:S(2)}) copy-start(f32[1344]{0:T(1024)} %param.24) | copy-start | bytes 16132
  375.8 7.3 %copy-start.9 = (f32[1344]{0:T(1024)S(1)}, f32[1344]{0:T(1024)}, u32[]{:S(2)}) copy-start(f32[1344]{0:T(1024)} %param.26) | copy-start | bytes 16132
  375.9 7.3 %copy-start.10 = (f32[1344]{0:T(1024)S(1)}, f32[1344]{0:T(1024)}, u32[]{:S(2)}) copy-start(f32[1344]{0:T(1024)} %param.25) | copy-start | bytes 16132
  376.9 35.7 %copy-start = (bf16[192,1280]{1,0:T(8,128)(2,1)}, bf16[192,1280]{1,0:T(8,128)(2,1)S(1)}, u32[]{:S(2)}) copy-start(bf16[192,1280]{1,0:T(8,128)(2,1)S(1)} %slice.29) | copy-start | bytes 1474564
  378.6 33.4 %all-to-all-start.1 = ((bf16[16,4,320]{2,0,1:T(8,128)(2,1)}), bf16[16,4,320]{2,0,1:T(8,128)(2,1)S(1)}, u32[]{:S(2)}, u32[]{:S(2)}) async-start(bf16[16,4,320]{2,0,1:T(8,128)(2,1)} %copy.61), calls=%async_computation.1 | async-start | bytes 98304 | tf_op jit(solution)/shard_map/all_to_all | solution.py:90
Sparse Core Ops, SparseCore 0:
  11.5 207.9 all-reduce.2
where the time goes:
time: 420 us; the launch traced here: 419 us
  waiting for transfers between devices  202 us (48%)
  blocking collectives  170 us (40%)
  between operations  17.7 us (4%)
  local copies, waits for them, and re-layouts  14 us (3%)
  starting transfers between devices  9.3 us (2%)
  other arithmetic  6.4 us (2%)
    psum x1, waiting for transfers between devices, body(): summed = lax.psum(local_flat.astype(jnp.float32), 'fsdp')  199 us
    psum x1, blocking collectives, body(): global_squares = lax.psum(local_squares, ('fsdp', 'tp'))  95.3 us
    all_gather x1, blocking collectives, body(): lax.all_gather(flat_new.astype(jnp.bfloat16), 'fsdp', axis=0, tiled=True)  51.2 us
    all_gather x1, blocking collectives, body(): lax.all_gather(o_block, 'tp', axis=0, tiled=True)  11.9 us
    all_gather x1, blocking collectives, body(): lax.all_gather(q_block, 'tp', axis=1, tiled=True)  11.9 us
  transfers between devices with their start and end apart: 3, of which 2 were waited for; matrix products, arithmetic and copies ran while one was open for 1% of the time, Pallas kernels for 0%

commit v1 on v0

v1 whole, which is shorter than its diff:
```python
import math

import jax
import jax.numpy as jnp
from jax import lax
from jax.sharding import Mesh
from jax.sharding import PartitionSpec as P

BETA_ONE = 0.9
BETA_TWO = 0.95
EPSILON = 1e-08
LEARN_RATE = 0.0053

FSDP = ("z", "y", "c")
CORES = 2
Y_SIZE = 8


def adam_update(weights_in, first_in, second_in, gradient, first_fix, second_fix, decay_rate):
    first_out = BETA_ONE * first_in + (1.0 - BETA_ONE) * gradient
    second_out = BETA_TWO * second_in + (1.0 - BETA_TWO) * gradient * gradient
    update = first_out / first_fix / (jnp.sqrt(second_out / second_fix) + EPSILON)
    weights_out = weights_in - LEARN_RATE * (update + decay_rate * weights_in)
    return (weights_out, first_out, second_out)


def fsdp_index():
    return (
        lax.axis_index("z") * (Y_SIZE * CORES)
        + lax.axis_index("y") * CORES
        + lax.axis_index("c")
    )


def body(
    q_grad,
    o_grad,
    norm_grad,
    emb_grad,
    flat_master,
    flat_first,
    flat_second,
    emb_master,
    emb_first,
    emb_second,
    norm_master,
    norm_first,
    norm_second,
    step_count,
):
    fsdp_count = lax.axis_size(FSDP)
    tp_count = lax.axis_size("tp")
    width = q_grad.shape[1]
    q_columns = q_grad.shape[2]
    entry_count = (
        2 * width * q_columns * tp_count
        + emb_grad.shape[0] * fsdp_count * width
        + norm_master.shape[0]
    )
    clip_limit = 0.5 * math.sqrt(entry_count)
    local_flat = jnp.concatenate([q_grad[0].reshape(-1), o_grad[0].reshape(-1)])
    piece_len = local_flat.shape[0] // fsdp_count
    pieces = lax.all_to_all(
        local_flat.reshape(fsdp_count, piece_len), FSDP, 0, 0, tiled=True
    )
    grad_piece = jnp.sum(pieces.astype(jnp.float32), axis=0)
    emb_piece = lax.all_to_all(emb_grad, "tp", split_axis=0, concat_axis=1, tiled=True).astype(
        jnp.float32
    )
    local_squares = jnp.sum(grad_piece * grad_piece) + jnp.sum(emb_piece * emb_piece)
    gains_local = norm_grad[0, 0]
    packed = jnp.concatenate([local_squares[None], gains_local])
    for axis in ("c", "tp", "y", "z"):
        packed = lax.psum(packed, axis)
    global_squares = packed[0]
    gain_sum = packed[1:]
    grad_norm = jnp.sqrt(global_squares + jnp.sum(gain_sum * gain_sum))
    clip_factor = jnp.minimum(jnp.float32(1.0), clip_limit / (grad_norm + 1e-06))
    step_value = step_count[0].astype(jnp.float32)
    first_fix = 1.0 - jnp.power(jnp.float32(BETA_ONE), step_value)
    second_fix = 1.0 - jnp.power(jnp.float32(BETA_TWO), step_value)
    flat_new, flat_one, flat_two = adam_update(
        flat_master[0],
        flat_first[0],
        flat_second[0],
        clip_factor * grad_piece,
        first_fix,
        second_fix,
        0.1,
    )
    emb_new, emb_one, emb_two = adam_update(
        emb_master, emb_first, emb_second, clip_factor * emb_piece, first_fix, second_fix, 0.1
    )
    norm_new, norm_one, norm_two = adam_update(
        norm_master, norm_first, norm_second, clip_factor * gain_sum, first_fix, second_fix, 0.0
    )
    gathered = lax.all_gather(flat_new.astype(jnp.bfloat16), "c", axis=0, tiled=False)
    gathered = lax.all_gather(gathered, ("z", "y"), axis=0, tiled=False).reshape(-1)
    q_weight = gathered[: width * q_columns].reshape(width, q_columns)
    o_weight = gathered[width * q_columns :].reshape(q_columns, width)
    block_rows = width // fsdp_count
    block_start = fsdp_index() * block_rows
    q_block = lax.dynamic_slice_in_dim(q_weight, block_start, block_rows, 0)
    o_block = lax.dynamic_slice_in_dim(o_weight, block_start, block_rows, 1)
    emb_rows = emb_new.astype(jnp.bfloat16)
    payload = jnp.concatenate([q_block.reshape(-1), o_block.reshape(-1), emb_rows.reshape(-1)])
    shared = lax.all_gather(payload, "tp", axis=0, tiled=False)
    q_len = block_rows * q_columns
    q_average = (
        shared[:, :q_len]
        .reshape(tp_count, block_rows, q_columns)
        .transpose(1, 0, 2)
        .reshape(block_rows, tp_count * q_columns)
    )
    o_average = shared[:, q_len : 2 * q_len].reshape(tp_count * q_columns, block_rows)
    emb_all = shared[:, 2 * q_len :].reshape(tp_count * emb_new.shape[0], width)
    emb_cols = width // tp_count
    emb_weight = lax.dynamic_slice_in_dim(emb_all, lax.axis_index("tp") * emb_cols, emb_cols, 1)
    return (
        flat_new[None, :],
        flat_one[None, :],
        flat_two[None, :],
        emb_new,
        emb_one,
        emb_two,
        norm_new,
        norm_one,
        norm_two,
        q_weight,
        o_weight,
        q_average,
        o_average,
        emb_weight,
    )


def solution(mesh):
    fsdp_count = mesh.shape["fsdp"]
    tp_count = mesh.shape["tp"]
    split = Mesh(
        mesh.devices.reshape(fsdp_count // (Y_SIZE * CORES), Y_SIZE, CORES, tp_count),
        ("z", "y", "c", "tp"),
    )
    both = FSDP + ("tp",)
    return jax.shard_map(
        body,
        mesh=split,
        in_specs=(
            P(FSDP, None, "tp"),
            P(FSDP, "tp", None),
            P(FSDP, "tp", None),
            P(FSDP, "tp"),
            P("tp", FSDP),
            P("tp", FSDP),
            P("tp", FSDP),
            P(both, None),
            P(both, None),
            P(both, None),
            P(),
            P(),
            P(),
            P(),
        ),
        out_specs=(
            P("tp", FSDP),
            P("tp", FSDP),
            P("tp", FSDP),
            P(both, None),
            P(both, None),
            P(both, None),
            P(),
            P(),
            P(),
            P(None, "tp"),
            P("tp", None),
            P(FSDP, None),
            P(None, FSDP),
            P(FSDP, "tp"),
        ),
        check_vma=False,
    )
```

time: 420 us -> 182 us (0.43)
  the two profiles are of different devices: /device:TPU:26 before, /device:TPU:8 now
where the time goes in v1:
time: 182 us; the launch traced here: 181 us
  blocking collectives  107 us (59%)
  waiting for transfers between devices  28.8 us (16%)
  starting transfers between devices  21.8 us (12%)
  local copies, waits for them, and re-layouts  11.6 us (6%)
  other arithmetic  7.56 us (4%)
  between operations  4.37 us (2%)
    all_gather x1, blocking collectives, body(): lax.all_gather(gathered, ('z', 'y'), axis=0, tiled=False).reshape(-1)  49 us
    psum x4, blocking collectives, body(): packed = lax.psum(packed, axis)  43.5 us
    all_to_all x1, waiting for transfers between devices, body(): lax.all_to_all(local_flat.reshape(fsdp_count, piece_len), FSDP, 0, 0, til...  28.6 us
    all_to_all x1, starting transfers between devices, body(): lax.all_to_all(local_flat.reshape(fsdp_count, piece_len), FSDP, 0, 0, til...  17.4 us
    all_gather x1, blocking collectives, body(): shared = lax.all_gather(payload, 'tp', axis=0, tiled=False)  12.5 us
    unnamed x32, local copies, waits for them, and re-layouts  5.25 us
    all_to_all x1, starting transfers between devices, body(): lax.all_to_all(emb_grad, 'tp', split_axis=0, concat_axis=1, tiled=True)  4.44 us
  transfers between devices with their start and end apart: 2, of which 2 were waited for; matrix products, arithmetic and copies ran while one was open for 3% of the time, Pallas kernels for 0%

profile of v1, /device:TPU:8, one launch (start us, length us, event | category | flops | bytes accessed | tf_op | source)
XLA Modules:
  0.0 181.0 jit_solution(17997149742384361667)
XLA Ops:
  0.6 0.0 copy-start.1
  0.7 4.4 %all-to-all-start.1 = ((bf16[4,16,320]{2,1,0:T(8,128)(2,1)}), bf16[4,16,320]{2,1,0:T(8,128)(2,1)S(1)}, u32[]{:S(2)}, u32[]{:S(2)}) async-start(bf16[4,16,320]{2,1,0:T(8,128)(2,1)} %bitcast.22), calls=%async_computation.1 | async-start | bytes 98304 | tf_op jit(solution)/shard_map/all_to_all | solution.py:67
  5.1 1.3 copy.44
  6.4 0.7 concatenate.14
  7.0 0.0 copy-done.1
  7.0 0.2 concatenate.15
  7.3 0.1 maximum_bitcast_fusion
  7.4 0.5 broadcast.70
  7.9 1.4 reduce.4
  9.2 0.0 copy-start.11
  9.3 1.2 reshape.135
  10.4 0.2 all-to-all-done.1
  10.6 17.4 %all-to-all-start = ((bf16[128,2,1920]{2,1,0:T(2,128)(2,1)}), bf16[128,2,1920]{2,1,0:T(2,128)(2,1)S(1)}, u32[]{:S(2)}, u32[]{:S(2)}) async-start(bf16[128,2,1920]{2,1,0:T(2,128)(2,1)} %reshape.135), calls=%async_computation | async-start | bytes 1966080 | tf_op jit(solution)/shard_map/all_to_all | solution.py:63
  28.7 0.0 copy-done.11
  28.8 0.6 fusion
  29.4 0.0 copy-start.5
  29.4 28.6 %all-to-all-done = bf16[128,2,1920]{2,1,0:T(2,128)(2,1)S(1)} async-done(((bf16[128,2,1920]{2,1,0:T(2,128)(2,1)}), bf16[128,2,1920]{2,1,0:T(2,128)(2,1)S(1)}, u32[]{:S(2)}, u32[]{:S(2)}) %all-to-all-start) | async-done | bytes 983072 | tf_op jit(solution)/shard_map/all_to_all | solution.py:63
  58.1 0.8 reshape.136
  58.9 1.9 %convert_reduce_fusion = f32[3840]{0:T(1024)S(1)} fusion(bf16[128,1,3840]{2,1,0:T(2,128)(2,1)S(1)} %reshape.136), kind=kLoop, calls=%fused_computation | loop fusion | flops 979200 | bytes 998400 | tf_op jit(solution)/shard_map/reduce_sum | solution.py:66
  60.8 0.6 multiply_reduce_fusion
  62.7 0.1 pad_maximum_fusion.1
  62.8 2.5 %psum.28 = f32[1345]{0:T(1024)S(1)} all-reduce(f32[1345]{0:T(1024)S(1)} %pad_maximum_fusion.1), channel_id=1, replica_groups=mesh['z'=8,'y'=8,'c'=2,'tp'=4] {'c'}, use_global_device_ids=true, to_apply=%region_3.0 | all-reduce | flops 1345 | bytes 10760 | tf_op jit(solution)/shard_map/psum | solution.py:74
  65.2 10.9 %psum.29 = f32[1345]{0:T(1024)S(1)} all-reduce(f32[1345]{0:T(1024)S(1)} %psum.28), channel_id=1, replica_groups=mesh['z'=8,'y'=8,'c'=2,'tp'=4] {'tp'}, use_global_device_ids=true, to_apply=%region_4.0 | all-reduce | flops 1345 | bytes 10760 | tf_op jit(solution)/shard_map/psum | solution.py:74
  76.1 14.5 %psum.30 = f32[1345]{0:T(1024)S(1)} all-reduce(f32[1345]{0:T(1024)S(1)} %psum.29), channel_id=1, replica_groups=mesh['z'=8,'y'=8,'c'=2,'tp'=4] {'y'}, use_global_device_ids=true, to_apply=%region_5.0 | all-reduce | flops 1345 | bytes 10760 | tf_op jit(solution)/shard_map/psum | solution.py:74
  90.6 15.7 %psum.31 = f32[1345]{0:T(1024)S(1)} all-reduce(f32[1345]{0:T(1024)S(1)} %psum.30), channel_id=1, replica_groups=mesh['z'=8,'y'=8,'c'=2,'tp'=4] {'z'}, use_global_device_ids=true, to_apply=%region_6.0 | all-reduce | flops 1345 | bytes 10760 | tf_op jit(solution)/shard_map/psum | solution.py:74
  106.3 0.5 slice.34
  106.8 0.7 multiply_reduce_fusion.1
  108.9 0.0 copy-done.5
  108.9 0.0 copy-done.6
  108.9 0.0 copy-done.7
  108.9 0.7 convert_bitcast_fusion
  109.6 1.8 %all-gather.2 = bf16[2,1,3840]{2,1,0:T(2,128)(2,1)S(1)} all-gather(bf16[1,1,3840]{2,1,0:T(2,128)(2,1)S(1)} %get-tuple-element.74), channel_id=1, replica_groups=mesh['z'=8,'y'=8,'c'=2,'tp'=4] {'c'}, dimensions={0}, use_global_device_ids=true | all-gather | bytes 23040 | tf_op jit(solution)/shard_map/all_gather | solution.py:97
  111.5 49.0 %all-gather.3 = bf16[64,2,3840]{2,1,0:T(2,128)(2,1)S(1)} all-gather(bf16[1,2,3840]{2,1,0:T(2,128)(2,1)S(1)} %bitcast.21), channel_id=2, replica_groups=mesh['z'=8,'y'=8,'c'=2,'tp'=4] {'z','y'}, dimensions={0}, use_global_device_ids=true | all-gather | bytes 998400 | tf_op jit(solution)/shard_map/all_gather | solution.py:98
  160.5 0.0 copy-start.3
  160.5 0.0 copy-start.4
  160.6 0.7 fusion.9
  161.2 0.7 reshape.107
  162.0 0.1 reshape.109
  162.1 0.3 reshape.108
  162.4 0.0 copy-start
  162.4 0.1 constant_dynamic-slice_fusion.1
  162.5 0.1 reshape.110
  162.7 0.1 mul.227
  162.8 0.0 copy-done.2
  162.8 0.0 copy-done.3
  162.9 0.0 copy-done.4
  162.9 0.8 fusion.5
  163.6 0.1 reshape.111
  163.7 0.1 reshape.126
  163.8 12.5 %all-gather.4 = bf16[4,1,24320]{2,1,0:T(2,128)(2,1)S(1)} all-gather(bf16[1,1,24320]{2,1,0:T(2,128)(2,1)S(1)} %reshape.126), channel_id=3, replica_groups=mesh['z'=8,'y'=8,'c'=2,'tp'=4] {'tp'}, dimensions={0}, use_global_device_ids=true | all-gather | bytes 243200 | tf_op jit(solution)/shard_map/all_gather | solution.py:107
  176.3 0.1 copy.54
  176.4 0.1 slice.40
  176.5 1.0 copy.48
  177.5 0.0 copy-done
  177.5 0.1 reshape.115
  177.6 0.4 reshape.114
  178.0 0.7 copy.49
  178.8 0.1 reshape.112
  178.9 0.7 reshape.113
  179.6 0.7 constant_dynamic-slice_fusion
  180.3 0.0 copy-done.8
  180.3 0.0 copy-done.9
  180.3 0.0 copy-done.10
  180.3 0.7 multiply_subtract_fusion.2
  (15 shorter events, 0.2 us)
Async XLA Ops:
  0.6 6.4 %copy-start.1 = (bf16[1,192,1280]{2,1,0:T(8,128)(2,1)S(1)}, bf16[1,192,1280]{2,1,0:T(8,128)(2,1)}, u32[]{:S(2)}) copy-start(bf16[1,192,1280]{2,1,0:T(8,128)(2,1)} %param.15) | copy-start | bytes 1474564
  0.7 10.0 %all-to-all-start.1 = ((bf16[4,16,320]{2,1,0:T(8,128)(2,1)}), bf16[4,16,320]{2,1,0:T(8,128)(2,1)S(1)}, u32[]{:S(2)}, u32[]{:S(2)}) async-start(bf16[4,16,320]{2,1,0:T(8,128)(2,1)} %bitcast.22), calls=%async_computation.1 | async-start | bytes 98304 | tf_op jit(solution)/shard_map/all_to_all | solution.py:67
  9.2 19.5 %copy-start.11 = (f32[1,1,1344]{2,1,0:T(1,128)S(1)}, f32[1,1,1344]{2,1,0:T(1,128)}, u32[]{:S(2)}) copy-start(f32[1,1,1344]{2,1,0:T(1,128)} %param.16) | copy-start | bytes 16132
  10.6 47.4 %all-to-all-start = ((bf16[128,2,1920]{2,1,0:T(2,128)(2,1)}), bf16[128,2,1920]{2,1,0:T(2,128)(2,1)S(1)}, u32[]{:S(2)}, u32[]{:S(2)}) async-start(bf16[128,2,1920]{2,1,0:T(2,128)(2,1)} %reshape.135), calls=%async_computation | async-start | bytes 1966080 | tf_op jit(solution)/shard_map/all_to_all | solution.py:63
  29.4 79.5 %copy-start.5 = (f32[1,3840]{1,0:T(1,128)S(1)}, f32[1,3840]{1,0:T(1,128)}, u32[]{:S(2)}) copy-start(f32[1,3840]{1,0:T(1,128)} %param.18) | copy-start | bytes 46084
  29.4 79.5 %copy-start.6 = (f32[1,3840]{1,0:T(1,128)S(1)}, f32[1,3840]{1,0:T(1,128)}, u32[]{:S(2)}) copy-start(f32[1,3840]{1,0:T(1,128)} %param.20) | copy-start | bytes 46084
  29.4 79.5 %copy-start.7 = (f32[1,3840]{1,0:T(1,128)S(1)}, f32[1,3840]{1,0:T(1,128)}, u32[]{:S(2)}) copy-start(f32[1,3840]{1,0:T(1,128)} %param.19) | copy-start | bytes 46084
  160.5 2.3 %copy-start.2 = (f32[16,1280]{1,0:T(8,128)S(1)}, f32[16,1280]{1,0:T(8,128)}, u32[]{:S(2)}) copy-start(f32[16,1280]{1,0:T(8,128)} %param.21) | copy-start | bytes 245764
  160.5 2.3 %copy-start.3 = (f32[16,1280]{1,0:T(8,128)S(1)}, f32[16,1280]{1,0:T(8,128)}, u32[]{:S(2)}) copy-start(f32[16,1280]{1,0:T(8,128)} %param.23) | copy-start | bytes 245764
  160.5 2.3 %copy-start.4 = (f32[16,1280]{1,0:T(8,128)S(1)}, f32[16,1280]{1,0:T(8,128)}, u32[]{:S(2)}) copy-start(f32[16,1280]{1,0:T(8,128)} %param.22) | copy-start | bytes 245764
  162.4 15.1 %copy-start = (bf16[192,1280]{1,0:T(8,128)(2,1)}, bf16[192,1280]{1,0:T(8,128)(2,1)S(1)}, u32[]{:S(2)}) copy-start(bf16[192,1280]{1,0:T(8,128)(2,1)S(1)} %reshape.108) | copy-start | bytes 1474564
  163.6 16.7 %copy-start.8 = (f32[1344]{0:T(1024)S(1)}, f32[1344]{0:T(1024)}, u32[]{:S(2)}) copy-start(f32[1344]{0:T(1024)} %param.24) | copy-start | bytes 16132
  163.6 16.7 %copy-start.9 = (f32[1344]{0:T(1024)S(1)}, f32[1344]{0:T(1024)}, u32[]{:S(2)}) copy-start(f32[1344]{0:T(1024)} %param.26) | copy-start | bytes 16132
  163.6 16.7 %copy-start.10 = (f32[1344]{0:T(1024)S(1)}, f32[1344]{0:T(1024)}, u32[]{:S(2)}) copy-start(f32[1344]{0:T(1024)} %param.25) | copy-start | bytes 16132

commit v2 on v1

--- a/solution.py
+++ b/solution.py
@@ -70,8 +70,10 @@
     local_squares = jnp.sum(grad_piece * grad_piece) + jnp.sum(emb_piece * emb_piece)
     gains_local = norm_grad[0, 0]
     packed = jnp.concatenate([local_squares[None], gains_local])
-    for axis in ("c", "tp", "y", "z"):
-        packed = lax.psum(packed, axis)
+    for axis in (("y", "c"), "z", "tp"):
+        count = lax.axis_size(axis)
+        copies = jnp.broadcast_to(packed[None], (count,) + packed.shape)
+        packed = jnp.sum(lax.all_to_all(copies, axis, 0, 0, tiled=True), axis=0)
     global_squares = packed[0]
     gain_sum = packed[1:]
     grad_norm = jnp.sqrt(global_squares + jnp.sum(gain_sum * gain_sum))
@@ -94,8 +96,8 @@
     norm_new, norm_one, norm_two = adam_update(
         norm_master, norm_first, norm_second, clip_factor * gain_sum, first_fix, second_fix, 0.0
     )
-    gathered = lax.all_gather(flat_new.astype(jnp.bfloat16), "c", axis=0, tiled=False)
-    gathered = lax.all_gather(gathered, ("z", "y"), axis=0, tiled=False).reshape(-1)
+    gathered = lax.all_gather(flat_new.astype(jnp.bfloat16), ("y", "c"), axis=0, tiled=False)
+    gathered = lax.all_gather(gathered, "z", axis=0, tiled=False).reshape(-1)
     q_weight = gathered[: width * q_columns].reshape(width, q_columns)
     o_weight = gathered[width * q_columns :].reshape(q_columns, width)
     block_rows = width // fsdp_count

time: 182 us -> 161 us (0.88)
  blocking collectives: 107 us -> 76.4 us
  waiting for transfers between devices: 28.8 us -> 34.2 us
  starting transfers between devices: 21.8 us -> 26.4 us
    psum x4 -> x0, blocking collectives: 43.5 us -> none  [body(): packed = lax.psum(packed, axis)]
    all_to_all x0 -> x2, blocking collectives: none -> 20.9 us  [body(): packed = jnp.sum(lax.all_to_all(copies, axis, 0, 0, tiled=True), axis=0)]
    all_gather x2, blocking collectives: 50.9 us -> 43 us  [the longest x1 26.6 us: body(): gathered = lax.all_gather(gathered, 'z', axis=0, tiled=False).reshape(-1)]
    all_to_all x0 -> x1, waiting for transfers between devices: none -> 4.66 us  [body(): packed = jnp.sum(lax.all_to_all(copies, axis, 0, 0, tiled=True), axis=0)]
    all_to_all x0 -> x1, starting transfers between devices: none -> 4.61 us  [body(): packed = jnp.sum(lax.all_to_all(copies, axis, 0, 0, tiled=True), axis=0)]
  transfers between devices with their start and end apart: 2 -> 3, of which waited for: 2 -> 3; matrix products, arithmetic and copies ran while one was open for 3% -> 4% of each run, Pallas kernels for 0% -> 0%
where the time goes in v2:
time: 161 us
  blocking collectives  76.4 us (47%)
  waiting for transfers between devices  34.2 us (21%)
  starting transfers between devices  26.4 us (16%)
  local copies, waits for them, and re-layouts  11.6 us (7%)
  other arithmetic  7.7 us (5%)
  between operations  4.36 us (3%)
    all_to_all x1, waiting for transfers between devices, body(): lax.all_to_all(local_flat.reshape(fsdp_count, piece_len), FSDP, 0, 0, til...  29.4 us
    all_gather x1, blocking collectives, body(): gathered = lax.all_gather(gathered, 'z', axis=0, tiled=False).reshape(-1)  26.6 us
    all_to_all x2, blocking collectives, body(): packed = jnp.sum(lax.all_to_all(copies, axis, 0, 0, tiled=True), axis=0)  20.9 us
    all_to_all x1, starting transfers between devices, body(): lax.all_to_all(local_flat.reshape(fsdp_count, piece_len), FSDP, 0, 0, til...  17.4 us
    all_gather x1, blocking collectives, body(): lax.all_gather(flat_new.astype(jnp.bfloat16), ('y', 'c'), axis=0, tiled=F...  16.4 us
    all_gather x1, blocking collectives, body(): shared = lax.all_gather(payload, 'tp', axis=0, tiled=False)  12.5 us
    unnamed x32, local copies, waits for them, and re-layouts  5.25 us
    all_to_all x1, waiting for transfers between devices, body(): packed = jnp.sum(lax.all_to_all(copies, axis, 0, 0, tiled=True), axis=0)  4.66 us
  transfers between devices with their start and end apart: 3, of which 3 were waited for; matrix products, arithmetic and copies ran while one was open for 4% of the time, Pallas kernels for 0%

profile of v2, /device:TPU:8, one launch (start us, length us, event | category | flops | bytes accessed | tf_op | source)
XLA Modules:
  0.0 160.8 jit_solution(17293533144932276652)
XLA Ops:
  0.6 0.0 copy-start.1
  0.7 4.4 %all-to-all-start.1 = ((bf16[4,16,320]{2,1,0:T(8,128)(2,1)}), bf16[4,16,320]{2,1,0:T(8,128)(2,1)S(1)}, u32[]{:S(2)}, u32[]{:S(2)}) async-start(bf16[4,16,320]{2,1,0:T(8,128)(2,1)} %bitcast.22), calls=%async_computation.1 | async-start | bytes 98304 | tf_op jit(solution)/shard_map/all_to_all | solution.py:67
  5.1 1.3 copy.56
  6.4 0.7 concatenate.14
  7.0 0.0 copy-done.1
  7.0 0.2 concatenate.15
  7.3 0.1 maximum_bitcast_fusion
  7.4 0.5 broadcast.79
  7.9 1.4 reduce.7
  9.2 0.0 copy-start.11
  9.3 1.2 reshape.146
  10.4 0.2 all-to-all-done.1
  10.6 17.4 %all-to-all-start = ((bf16[128,2,1920]{2,1,0:T(2,128)(2,1)}), bf16[128,2,1920]{2,1,0:T(2,128)(2,1)S(1)}, u32[]{:S(2)}, u32[]{:S(2)}) async-start(bf16[128,2,1920]{2,1,0:T(2,128)(2,1)} %reshape.146), calls=%async_computation | async-start | bytes 1966080 | tf_op jit(solution)/shard_map/all_to_all | solution.py:63
  28.0 0.0 copy-done.11
  28.0 0.6 fusion
  28.7 29.4 %all-to-all-done = bf16[128,2,1920]{2,1,0:T(2,128)(2,1)S(1)} async-done(((bf16[128,2,1920]{2,1,0:T(2,128)(2,1)}), bf16[128,2,1920]{2,1,0:T(2,128)(2,1)S(1)}, u32[]{:S(2)}, u32[]{:S(2)}) %all-to-all-start) | async-done | bytes 983072 | tf_op jit(solution)/shard_map/all_to_all | solution.py:63
  58.1 0.8 reshape.147
  58.9 0.0 copy-start.5
  58.9 0.0 copy-start.6
  58.9 0.0 copy-start.7
  58.9 1.9 %convert_reduce_fusion = f32[3840]{0:T(1024)S(1)} fusion(bf16[128,1,3840]{2,1,0:T(2,128)(2,1)S(1)} %reshape.147), kind=kLoop, calls=%fused_computation | loop fusion | flops 979200 | bytes 998400 | tf_op jit(solution)/shard_map/reduce_sum | solution.py:66
  60.8 0.6 multiply_reduce_fusion
  62.8 0.1 pad_maximum_fusion.1
  62.8 0.1 broadcast_in_dim.9
  62.9 10.4 %all_to_all.40 = f32[16,1,1345]{2,1,0:T(1,128)S(1)} all-to-all(f32[16,1,1345]{2,1,0:T(1,128)S(1)} %broadcast_in_dim.9), channel_id=1, replica_groups=mesh['z'=8,'y'=8,'c'=2,'tp'=4] {'y','c'}, dimensions={0} | all-to-all | bytes 172160 | tf_op jit(solution)/shard_map/all_to_all | solution.py:76
  73.2 0.1 reduce_sum.66
  73.3 10.5 %all_to_all.41 = f32[8,1,1345]{2,1,0:T(1,128)S(1)} all-to-all(f32[8,1,1345]{2,1,0:T(1,128)S(1)} %broadcast_in_dim.10), channel_id=1, replica_groups=mesh['z'=8,'y'=8,'c'=2,'tp'=4] {'z'}, dimensions={0} | all-to-all | bytes 86080 | tf_op jit(solution)/shard_map/all_to_all | solution.py:76
  83.9 0.6 broadcast_in_dim.11
  84.5 4.6 %all-to-all-start.4 = ((f32[4,1,1345]{2,1,0:T(1,128)}), f32[4,1,1345]{2,1,0:T(1,128)S(1)}, u32[]{:S(2)}, u32[]{:S(2)}) async-start(f32[4,1,1345]{2,1,0:T(1,128)} %broadcast_in_dim.11), calls=%async_computation.4 | async-start | bytes 45056 | tf_op jit(solution)/shard_map/all_to_all | solution.py:76
  89.9 4.7 %all-to-all-done.4 = f32[4,1,1345]{2,1,0:T(1,128)S(1)} async-done(((f32[4,1,1345]{2,1,0:T(1,128)}), f32[4,1,1345]{2,1,0:T(1,128)S(1)}, u32[]{:S(2)}, u32[]{:S(2)}) %all-to-all-start.4) | async-done | bytes 21552 | tf_op jit(solution)/shard_map/all_to_all | solution.py:76
  94.6 0.5 slice.32
  95.1 0.7 multiply_reduce_fusion.1
  97.1 0.0 copy-done.5
  97.2 0.0 copy-done.6
  97.2 0.0 copy-done.7
  97.2 0.7 convert_bitcast_fusion
  97.9 16.4 %all-gather.2 = bf16[16,1,3840]{2,1,0:T(2,128)(2,1)S(1)} all-gather(bf16[1,1,3840]{2,1,0:T(2,128)(2,1)S(1)} %get-tuple-element.102), channel_id=1, replica_groups=mesh['z'=8,'y'=8,'c'=2,'tp'=4] {'y','c'}, dimensions={0}, use_global_device_ids=true | all-gather | bytes 130560 | tf_op jit(solution)/shard_map/all_gather | solution.py:99
  114.3 26.6 %all-gather = bf16[128,3840]{1,0:T(8,128)(2,1)S(1)} all-gather(bf16[16,3840]{1,0:T(8,128)(2,1)S(1)} %bitcast.20), channel_id=2, replica_groups=mesh['z'=8,'y'=8,'c'=2,'tp'=4] {'z'}, dimensions={0}, use_global_device_ids=true | all-gather | bytes 1105920 | tf_op jit(solution)/shard_map/all_gather | solution.py:100
  140.9 0.1 fusion.9
  141.0 0.8 reshape.125
  141.8 0.1 reshape.127
  141.9 0.2 reshape.126
  142.1 0.0 copy-start
  142.2 0.1 constant_dynamic-slice_fusion.1
  142.3 0.1 reshape.128
  142.5 0.1 mul.227
  142.6 0.0 copy-done.2
  142.6 0.0 copy-done.3
  142.6 0.0 copy-done.4
  142.6 0.8 fusion.5
  143.4 0.1 reshape.129
  143.5 0.1 reshape.142
  143.5 12.5 %all-gather.3 = bf16[4,1,24320]{2,1,0:T(2,128)(2,1)S(1)} all-gather(bf16[1,1,24320]{2,1,0:T(2,128)(2,1)S(1)} %reshape.142), channel_id=3, replica_groups=mesh['z'=8,'y'=8,'c'=2,'tp'=4] {'tp'}, dimensions={0}, use_global_device_ids=true | all-gather | bytes 243200 | tf_op jit(solution)/shard_map/all_gather | solution.py:109
  156.1 0.1 copy.74
  156.2 0.1 slice.38
  156.3 1.0 copy.63
  157.3 0.1 reshape.133
  157.4 0.4 reshape.132
  157.8 0.7 copy.64
  158.5 0.1 reshape.130
  158.6 0.7 reshape.131
  159.3 0.7 constant_dynamic-slice_fusion
  160.1 0.0 copy-done.8
  160.1 0.7 multiply_subtract_fusion.2
  (21 shorter events, 0.3 us)
Async XLA Ops:
  0.6 6.4 %copy-start.1 = (bf16[1,192,1280]{2,1,0:T(8,128)(2,1)S(1)}, bf16[1,192,1280]{2,1,0:T(8,128)(2,1)}, u32[]{:S(2)}) copy-start(bf16[1,192,1280]{2,1,0:T(8,128)(2,1)} %param.15) | copy-start | bytes 1474564
  0.7 10.0 %all-to-all-start.1 = ((bf16[4,16,320]{2,1,0:T(8,128)(2,1)}), bf16[4,16,320]{2,1,0:T(8,128)(2,1)S(1)}, u32[]{:S(2)}, u32[]{:S(2)}) async-start(bf16[4,16,320]{2,1,0:T(8,128)(2,1)} %bitcast.22), calls=%async_computation.1 | async-start | bytes 98304 | tf_op jit(solution)/shard_map/all_to_all | solution.py:67
  9.2 18.8 %copy-start.11 = (f32[1,1,1344]{2,1,0:T(1,128)S(1)}, f32[1,1,1344]{2,1,0:T(1,128)}, u32[]{:S(2)}) copy-start(f32[1,1,1344]{2,1,0:T(1,128)} %param.16) | copy-start | bytes 16132
  10.6 47.4 %all-to-all-start = ((bf16[128,2,1920]{2,1,0:T(2,128)(2,1)}), bf16[128,2,1920]{2,1,0:T(2,128)(2,1)S(1)}, u32[]{:S(2)}, u32[]{:S(2)}) async-start(bf16[128,2,1920]{2,1,0:T(2,128)(2,1)} %reshape.146), calls=%async_computation | async-start | bytes 1966080 | tf_op jit(solution)/shard_map/all_to_all | solution.py:63
  58.9 38.3 %copy-start.5 = (f32[1,3840]{1,0:T(1,128)S(1)}, f32[1,3840]{1,0:T(1,128)}, u32[]{:S(2)}) copy-start(f32[1,3840]{1,0:T(1,128)} %param.18) | copy-start | bytes 46084
  58.9 38.3 %copy-start.6 = (f32[1,3840]{1,0:T(1,128)S(1)}, f32[1,3840]{1,0:T(1,128)}, u32[]{:S(2)}) copy-start(f32[1,3840]{1,0:T(1,128)} %param.20) | copy-start | bytes 46084
  58.9 38.3 %copy-start.7 = (f32[1,3840]{1,0:T(1,128)S(1)}, f32[1,3840]{1,0:T(1,128)}, u32[]{:S(2)}) copy-start(f32[1,3840]{1,0:T(1,128)} %param.19) | copy-start | bytes 46084
  84.5 10.0 %all-to-all-start.4 = ((f32[4,1,1345]{2,1,0:T(1,128)}), f32[4,1,1345]{2,1,0:T(1,128)S(1)}, u32[]{:S(2)}, u32[]{:S(2)}) async-start(f32[4,1,1345]{2,1,0:T(1,128)} %broadcast_in_dim.11), calls=%async_computation.4 | async-start | bytes 45056 | tf_op jit(solution)/shard_map/all_to_all | solution.py:76
  140.9 1.7 %copy-start.2 = (f32[16,1280]{1,0:T(8,128)S(1)}, f32[16,1280]{1,0:T(8,128)}, u32[]{:S(2)}) copy-start(f32[16,1280]{1,0:T(8,128)} %param.21) | copy-start | bytes 245764
  140.9 1.7 %copy-start.3 = (f32[16,1280]{1,0:T(8,128)S(1)}, f32[16,1280]{1,0:T(8,128)}, u32[]{:S(2)}) copy-start(f32[16,1280]{1,0:T(8,128)} %param.23) | copy-start | bytes 245764
  140.9 1.7 %copy-start.4 = (f32[16,1280]{1,0:T(8,128)S(1)}, f32[16,1280]{1,0:T(8,128)}, u32[]{:S(2)}) copy-start(f32[16,1280]{1,0:T(8,128)} %param.22) | copy-start | bytes 245764
  142.1 15.1 %copy-start = (bf16[192,1280]{1,0:T(8,128)(2,1)}, bf16[192,1280]{1,0:T(8,128)(2,1)S(1)}, u32[]{:S(2)}) copy-start(bf16[192,1280]{1,0:T(8,128)(2,1)S(1)} %reshape.126) | copy-start | bytes 1474564
  143.4 16.7 %copy-start.8 = (f32[1344]{0:T(1024)S(1)}, f32[1344]{0:T(1024)}, u32[]{:S(2)}) copy-start(f32[1344]{0:T(1024)} %param.24) | copy-start | bytes 16132
  143.4 16.7 %copy-start.9 = (f32[1344]{0:T(1024)S(1)}, f32[1344]{0:T(1024)}, u32[]{:S(2)}) copy-start(f32[1344]{0:T(1024)} %param.26) | copy-start | bytes 16132
  143.4 16.7 %copy-start.10 = (f32[1344]{0:T(1024)S(1)}, f32[1344]{0:T(1024)}, u32[]{:S(2)}) copy-start(f32[1344]{0:T(1024)} %param.25) | copy-start | bytes 16132

commit v3 on v2

--- a/solution.py
+++ b/solution.py
@@ -60,17 +60,21 @@
     clip_limit = 0.5 * math.sqrt(entry_count)
     local_flat = jnp.concatenate([q_grad[0].reshape(-1), o_grad[0].reshape(-1)])
     piece_len = local_flat.shape[0] // fsdp_count
-    pieces = lax.all_to_all(
-        local_flat.reshape(fsdp_count, piece_len), FSDP, 0, 0, tiled=True
+    core_count = lax.axis_size("c")
+    halves = lax.all_to_all(
+        local_flat.reshape(fsdp_count // core_count, core_count, piece_len), "c", 1, 1, tiled=True
     )
-    grad_piece = jnp.sum(pieces.astype(jnp.float32), axis=0)
+    partial = jnp.sum(halves.astype(jnp.float32), axis=1)
+    pieces = lax.all_to_all(partial, ("z", "y"), 0, 0, tiled=True)
+    grad_piece = jnp.sum(pieces, axis=0)
     emb_piece = lax.all_to_all(emb_grad, "tp", split_axis=0, concat_axis=1, tiled=True).astype(
         jnp.float32
     )
-    local_squares = jnp.sum(grad_piece * grad_piece) + jnp.sum(emb_piece * emb_piece)
+    emb_float = emb_grad.astype(jnp.float32)
+    local_squares = jnp.sum(grad_piece * grad_piece) + jnp.sum(emb_float * emb_float)
     gains_local = norm_grad[0, 0]
     packed = jnp.concatenate([local_squares[None], gains_local])
-    for axis in (("y", "c"), "z", "tp"):
+    for axis in (("y", "c"), ("z", "tp")):
         count = lax.axis_size(axis)
         copies = jnp.broadcast_to(packed[None], (count,) + packed.shape)
         packed = jnp.sum(lax.all_to_all(copies, axis, 0, 0, tiled=True), axis=0)

time: 161 us -> 160 us (level)
  waiting for transfers between devices: 34.2 us -> 37.9 us
  blocking collectives: 76.4 us -> 73 us
    all_to_all x2 -> x1, blocking collectives: 20.9 us -> 12.1 us  [body(): packed = jnp.sum(lax.all_to_all(copies, axis, 0, 0, tiled=True), axis=0)]
    all_to_all x1, waiting for transfers between devices: 4.66 us -> 11.2 us  [body(): packed = jnp.sum(lax.all_to_all(copies, axis, 0, 0, tiled=True), axis=0)]
    all_to_all x0 -> x1, blocking collectives: none -> 4.52 us  [body(): lax.all_to_all(local_flat.reshape(fsdp_count // core_count, core_count, p...]
    all_to_all x1, waiting for transfers between devices: 29.4 us -> 26.7 us  [body(): pieces = lax.all_to_all(partial, ('z', 'y'), 0, 0, tiled=True)]
    unnamed x32 -> x30, local copies, waits for them, and re-layouts: 5.25 us -> 3.41 us
  transfers between devices with their start and end apart: 3 -> 3, of which waited for: 3 -> 2; matrix products, arithmetic and copies ran while one was open for 4% -> 3% of each run, Pallas kernels for 0% -> 0%
where the time goes in v3:
time: 160 us; the launch traced here: 159 us
  blocking collectives  73 us (46%)
  waiting for transfers between devices  37.9 us (24%)
  starting transfers between devices  25.5 us (16%)
  local copies, waits for them, and re-layouts  11.2 us (7%)
  other arithmetic  7.19 us (4%)
  between operations  4.39 us (3%)
    all_to_all x1, waiting for transfers between devices, body(): pieces = lax.all_to_all(partial, ('z', 'y'), 0, 0, tiled=True)  26.7 us
    all_gather x1, blocking collectives, body(): gathered = lax.all_gather(gathered, 'z', axis=0, tiled=False).reshape(-1)  26.5 us
    all_to_all x1, starting transfers between devices, body(): pieces = lax.all_to_all(partial, ('z', 'y'), 0, 0, tiled=True)  16.7 us
    all_gather x1, blocking collectives, body(): lax.all_gather(flat_new.astype(jnp.bfloat16), ('y', 'c'), axis=0, tiled=F...  16.5 us
    all_gather x1, blocking collectives, body(): shared = lax.all_gather(payload, 'tp', axis=0, tiled=False)  13.3 us
    all_to_all x1, blocking collectives, body(): packed = jnp.sum(lax.all_to_all(copies, axis, 0, 0, tiled=True), axis=0)  12.1 us
    all_to_all x1, waiting for transfers between devices, body(): packed = jnp.sum(lax.all_to_all(copies, axis, 0, 0, tiled=True), axis=0)  11.2 us
    all_to_all x1, starting transfers between devices, body(): packed = jnp.sum(lax.all_to_all(copies, axis, 0, 0, tiled=True), axis=0)  5.48 us
  transfers between devices with their start and end apart: 3, of which 2 were waited for; matrix products, arithmetic and copies ran while one was open for 3% of the time, Pallas kernels for 0%

profile of v3, /device:TPU:8, one launch (start us, length us, event | category | flops | bytes accessed | tf_op | source)
XLA Modules:
  0.0 159.2 jit_solution(10259803394664846084)
XLA Ops:
  0.6 0.0 copy-start.1
  0.7 1.3 copy.56
  2.0 0.7 concatenate.14
  2.7 0.0 copy-done.1
  2.7 0.3 concatenate.15
  3.0 1.3 pad_maximum_fusion
  4.3 0.1 copy.57
  4.4 4.5 %all_to_all.39 = bf16[64,2,3840]{2,0,1:T(8,128)(2,1)S(1)} all-to-all(bf16[64,2,3840]{2,0,1:T(8,128)(2,1)S(1)} %copy.57), channel_id=1, replica_groups=mesh['z'=8,'y'=8,'c'=2,'tp'=4] {'c'}, dimensions={1} | all-to-all | bytes 1966080 | tf_op jit(solution)/shard_map/all_to_all | solution.py:64
  8.9 0.1 convert_reduce_fusion
  9.1 1.6 %all_to_all.28 = f32[64,1,3840]{2,1,0:T(1,128)} reshape(f32[64,3840]{1,0:T(8,128)S(1)} %convert_reduce_fusion) | data formatting | bytes 1966080 | tf_op jit(solution)/shard_map/all_to_all | solution.py:68
  10.7 16.7 %all-to-all-start.1 = ((f32[64,1,3840]{2,1,0:T(1,128)}), f32[64,1,3840]{2,1,0:T(1,128)S(1)}, u32[]{:S(2)}, u32[]{:S(2)}) async-start(f32[64,1,3840]{2,1,0:T(1,128)} %all_to_all.28), calls=%async_computation.1 | async-start | bytes 1966080 | tf_op jit(solution)/shard_map/all_to_all | solution.py:68
  27.4 0.0 copy-done.11
  27.4 1.4 multiply_reduce_fusion
  28.9 26.7 %all-to-all-done.1 = f32[64,1,3840]{2,1,0:T(1,128)S(1)} async-done(((f32[64,1,3840]{2,1,0:T(1,128)}), f32[64,1,3840]{2,1,0:T(1,128)S(1)}, u32[]{:S(2)}, u32[]{:S(2)}) %all-to-all-start.1) | async-done | bytes 983072 | tf_op jit(solution)/shard_map/all_to_all | solution.py:68
  55.6 0.6 reduce_sum.64
  56.2 0.6 multiply_reduce_fusion.1
  58.1 0.1 pad_maximum_fusion.2
  58.2 0.1 broadcast_in_dim.7
  58.2 12.1 %all_to_all.40 = f32[16,1,1345]{2,1,0:T(1,128)S(1)} all-to-all(f32[16,1,1345]{2,1,0:T(1,128)S(1)} %broadcast_in_dim.7), channel_id=1, replica_groups=mesh['z'=8,'y'=8,'c'=2,'tp'=4] {'y','c'}, dimensions={0} | all-to-all | bytes 172160 | tf_op jit(solution)/shard_map/all_to_all | solution.py:80
  70.3 0.1 reduce_sum.67
  70.4 0.8 broadcast_in_dim.8
  71.2 5.5 %all-to-all-start.3 = ((f32[32,1,1345]{2,1,0:T(1,128)}), f32[32,1,1345]{2,1,0:T(1,128)S(1)}, u32[]{:S(2)}, u32[]{:S(2)}) async-start(f32[32,1,1345]{2,1,0:T(1,128)} %broadcast_in_dim.8), calls=%async_computation.3 | async-start | bytes 360448 | tf_op jit(solution)/shard_map/all_to_all | solution.py:80
  77.4 11.2 %all-to-all-done.3 = f32[32,1,1345]{2,1,0:T(1,128)S(1)} async-done(((f32[32,1,1345]{2,1,0:T(1,128)}), f32[32,1,1345]{2,1,0:T(1,128)S(1)}, u32[]{:S(2)}, u32[]{:S(2)}) %all-to-all-start.3) | async-done | bytes 172192 | tf_op jit(solution)/shard_map/all_to_all | solution.py:80
  88.6 3.3 %all-to-all-start.4 = ((bf16[4,16,320]{2,1,0:T(8,128)(2,1)}), bf16[4,16,320]{2,1,0:T(8,128)(2,1)S(1)}, u32[]{:S(2)}, u32[]{:S(2)}) async-start(bf16[4,16,320]{2,1,0:T(8,128)(2,1)} %bitcast.4), calls=%async_computation.4 | async-start | bytes 98304 | tf_op jit(solution)/shard_map/all_to_all | solution.py:70
  91.9 0.1 reduce_sum.68
  92.0 0.5 slice.32
  92.5 0.7 multiply_reduce_fusion.2
  94.6 0.0 copy-done.5
  94.6 0.7 convert_bitcast_fusion
  95.4 16.5 %all-gather.2 = bf16[16,1,3840]{2,1,0:T(2,128)(2,1)S(1)} all-gather(bf16[1,1,3840]{2,1,0:T(2,128)(2,1)S(1)} %get-tuple-element.102), channel_id=1, replica_groups=mesh['z'=8,'y'=8,'c'=2,'tp'=4] {'y','c'}, dimensions={0}, use_global_device_ids=true | all-gather | bytes 130560 | tf_op jit(solution)/shard_map/all_gather | solution.py:103
  111.9 26.5 %all-gather = bf16[128,3840]{1,0:T(8,128)(2,1)S(1)} all-gather(bf16[16,3840]{1,0:T(8,128)(2,1)S(1)} %bitcast.18), channel_id=2, replica_groups=mesh['z'=8,'y'=8,'c'=2,'tp'=4] {'z'}, dimensions={0}, use_global_device_ids=true | all-gather | bytes 1105920 | tf_op jit(solution)/shard_map/all_gather | solution.py:104
  138.4 0.1 fusion.7
  138.5 0.8 reshape.118
  139.3 0.0 copy-start.2
  139.3 0.0 copy-start.3
  139.3 0.0 copy-start.4
  139.3 0.2 reshape.119
  139.5 0.0 copy-start
  139.6 0.1 constant_dynamic-slice_fusion.1
  139.7 0.1 reshape.120
  139.8 0.1 reshape.121
  139.9 0.0 all-to-all-done.4
  140.0 0.1 mul.225
  140.1 0.0 copy-done.2
  140.2 0.0 copy-done.3
  140.2 0.0 copy-done.4
  140.2 0.8 fusion.3
  141.0 0.1 reshape.122
  141.1 0.1 reshape.135
  141.2 13.3 %all-gather.3 = bf16[4,1,24320]{2,1,0:T(2,128)(2,1)S(1)} all-gather(bf16[1,1,24320]{2,1,0:T(2,128)(2,1)S(1)} %reshape.135), channel_id=3, replica_groups=mesh['z'=8,'y'=8,'c'=2,'tp'=4] {'tp'}, dimensions={0}, use_global_device_ids=true | all-gather | bytes 243200 | tf_op jit(solution)/shard_map/all_gather | solution.py:113
  154.5 0.1 copy.72
  154.6 0.1 slice.38
  154.7 0.0 copy-start.8
  154.7 0.0 copy-start.9
  154.7 0.0 copy-start.10
  154.7 1.0 copy.62
  155.7 0.1 reshape.126
  155.8 0.4 reshape.125
  156.2 0.7 copy.63
  157.0 0.1 reshape.123
  157.1 0.7 reshape.124
  157.8 0.7 constant_dynamic-slice_fusion
  158.5 0.0 copy-done.9
  158.5 0.7 multiply_subtract_fusion.2
  (18 shorter events, 0.2 us)
Async XLA Ops:
  0.6 2.1 %copy-start.1 = (bf16[1,192,1280]{2,1,0:T(8,128)(2,1)S(1)}, bf16[1,192,1280]{2,1,0:T(8,128)(2,1)}, u32[]{:S(2)}) copy-start(bf16[1,192,1280]{2,1,0:T(8,128)(2,1)} %param.15) | copy-start | bytes 1474564
  10.7 16.7 %copy-start.11 = (f32[1,1,1344]{2,1,0:T(1,128)S(1)}, f32[1,1,1344]{2,1,0:T(1,128)}, u32[]{:S(2)}) copy-start(f32[1,1,1344]{2,1,0:T(1,128)} %param.16) | copy-start | bytes 16132
  10.7 44.9 %all-to-all-start.1 = ((f32[64,1,3840]{2,1,0:T(1,128)}), f32[64,1,3840]{2,1,0:T(1,128)S(1)}, u32[]{:S(2)}, u32[]{:S(2)}) async-start(f32[64,1,3840]{2,1,0:T(1,128)} %all_to_all.28), calls=%async_computation.1 | async-start | bytes 1966080 | tf_op jit(solution)/shard_map/all_to_all | solution.py:68
  28.9 65.7 %copy-start.5 = (f32[1,3840]{1,0:T(1,128)S(1)}, f32[1,3840]{1,0:T(1,128)}, u32[]{:S(2)}) copy-start(f32[1,3840]{1,0:T(1,128)} %param.18) | copy-start | bytes 46084
  28.9 65.7 %copy-start.6 = (f32[1,3840]{1,0:T(1,128)S(1)}, f32[1,3840]{1,0:T(1,128)}, u32[]{:S(2)}) copy-start(f32[1,3840]{1,0:T(1,128)} %param.20) | copy-start | bytes 46084
  28.9 65.8 %copy-start.7 = (f32[1,3840]{1,0:T(1,128)S(1)}, f32[1,3840]{1,0:T(1,128)}, u32[]{:S(2)}) copy-start(f32[1,3840]{1,0:T(1,128)} %param.19) | copy-start | bytes 46084
  71.2 17.4 %all-to-all-start.3 = ((f32[32,1,1345]{2,1,0:T(1,128)}), f32[32,1,1345]{2,1,0:T(1,128)S(1)}, u32[]{:S(2)}, u32[]{:S(2)}) async-start(f32[32,1,1345]{2,1,0:T(1,128)} %broadcast_in_dim.8), calls=%async_computation.3 | async-start | bytes 360448 | tf_op jit(solution)/shard_map/all_to_all | solution.py:80
  88.6 51.3 %all-to-all-start.4 = ((bf16[4,16,320]{2,1,0:T(8,128)(2,1)}), bf16[4,16,320]{2,1,0:T(8,128)(2,1)S(1)}, u32[]{:S(2)}, u32[]{:S(2)}) async-start(bf16[4,16,320]{2,1,0:T(8,128)(2,1)} %bitcast.4), calls=%async_computation.4 | async-start | bytes 98304 | tf_op jit(solution)/shard_map/all_to_all | solution.py:70
  139.3 0.9 copy-start.2
  139.3 0.9 copy-start.3
  139.3 0.9 copy-start.4
  139.5 15.0 %copy-start = (bf16[192,1280]{1,0:T(8,128)(2,1)}, bf16[192,1280]{1,0:T(8,128)(2,1)S(1)}, u32[]{:S(2)}) copy-start(bf16[192,1280]{1,0:T(8,128)(2,1)S(1)} %reshape.119) | copy-start | bytes 1474564
  154.7 3.8 %copy-start.8 = (f32[1344]{0:T(1024)S(1)}, f32[1344]{0:T(1024)}, u32[]{:S(2)}) copy-start(f32[1344]{0:T(1024)} %param.24) | copy-start | bytes 16132
  154.7 3.8 %copy-start.9 = (f32[1344]{0:T(1024)S(1)}, f32[1344]{0:T(1024)}, u32[]{:S(2)}) copy-start(f32[1344]{0:T(1024)} %param.26) | copy-start | bytes 16132
  154.7 3.8 %copy-start.10 = (f32[1344]{0:T(1024)S(1)}, f32[1344]{0:T(1024)}, u32[]{:S(2)}) copy-start(f32[1344]{0:T(1024)} %param.25) | copy-start | bytes 16132

commit v4 on v3

--- a/solution.py
+++ b/solution.py
@@ -67,17 +67,30 @@
     partial = jnp.sum(halves.astype(jnp.float32), axis=1)
     pieces = lax.all_to_all(partial, ("z", "y"), 0, 0, tiled=True)
     grad_piece = jnp.sum(pieces, axis=0)
-    emb_piece = lax.all_to_all(emb_grad, "tp", split_axis=0, concat_axis=1, tiled=True).astype(
-        jnp.float32
-    )
     emb_float = emb_grad.astype(jnp.float32)
     local_squares = jnp.sum(grad_piece * grad_piece) + jnp.sum(emb_float * emb_float)
     gains_local = norm_grad[0, 0]
     packed = jnp.concatenate([local_squares[None], gains_local])
-    for axis in (("y", "c"), ("z", "tp")):
+    def spread(values, axis):
         count = lax.axis_size(axis)
-        copies = jnp.broadcast_to(packed[None], (count,) + packed.shape)
-        packed = jnp.sum(lax.all_to_all(copies, axis, 0, 0, tiled=True), axis=0)
+        copies = jnp.broadcast_to(values[None], (count,) + values.shape)
+        return jnp.sum(lax.all_to_all(copies, axis, 0, 0, tiled=True), axis=0)
+
+    packed = spread(packed, ("y", "c"))
+    emb_blocks = emb_float.reshape(tp_count, -1)
+    with_emb = jnp.concatenate(
+        [jnp.broadcast_to(packed[None], (tp_count,) + packed.shape), emb_blocks], axis=1
+    )
+    received = lax.all_to_all(with_emb, "tp", 0, 0, tiled=True)
+    packed = jnp.sum(received[:, : packed.shape[0]], axis=0)
+    emb_rows_count = emb_grad.shape[0] // tp_count
+    emb_piece = (
+        received[:, packed.shape[0] :]
+        .reshape(tp_count, emb_rows_count, emb_grad.shape[1])
+        .transpose(1, 0, 2)
+        .reshape(emb_rows_count, tp_count * emb_grad.shape[1])
+    )
+    packed = spread(packed, "z")
     global_squares = packed[0]
     gain_sum = packed[1:]
     grad_norm = jnp.sqrt(global_squares + jnp.sum(gain_sum * gain_sum))

time: 160 us -> 161 us (level)
  waiting for transfers between devices: 37.9 us -> 41.4 us
  blocking collectives: 73 us -> 70 us
    all_to_all x2, waiting for transfers between devices: 11.2 us -> 13.9 us  [spread(): return jnp.sum(lax.all_to_all(copies, axis, 0, 0, tiled=True), axis=0)]
    all_to_all x1, blocking collectives: 12.1 us -> 9.93 us  [body(): received = lax.all_to_all(with_emb, 'tp', 0, 0, tiled=True)]
    unnamed x30 -> x33, local copies, waits for them, and re-layouts: 3.41 us -> 3.37 us
  transfers between devices with their start and end apart: 3 -> 3, of which waited for: 2 -> 3; matrix products, arithmetic and copies ran while one was open for 3% -> 0% of each run, Pallas kernels for 0% -> 0%
where the time goes in v4:
time: 161 us; the launch traced here: 160 us
  blocking collectives  70 us (43%)
  waiting for transfers between devices  41.4 us (26%)
  starting transfers between devices  25.7 us (16%)
  local copies, waits for them, and re-layouts  12 us (7%)
  other arithmetic  6.52 us (4%)
  between operations  4.44 us (3%)
    all_to_all x1, waiting for transfers between devices, body(): pieces = lax.all_to_all(partial, ('z', 'y'), 0, 0, tiled=True)  27.5 us
    all_gather x1, blocking collectives, body(): gathered = lax.all_gather(gathered, 'z', axis=0, tiled=False).reshape(-1)  26.6 us
    all_to_all x1, starting transfers between devices, body(): pieces = lax.all_to_all(partial, ('z', 'y'), 0, 0, tiled=True)  16.7 us
    all_gather x1, blocking collectives, body(): lax.all_gather(flat_new.astype(jnp.bfloat16), ('y', 'c'), axis=0, tiled=F...  16.4 us
    all_to_all x2, waiting for transfers between devices, spread(): return jnp.sum(lax.all_to_all(copies, axis, 0, 0, tiled=True), axis=0)  13.9 us
    all_gather x1, blocking collectives, body(): shared = lax.all_gather(payload, 'tp', axis=0, tiled=False)  12.5 us
    all_to_all x1, blocking collectives, body(): received = lax.all_to_all(with_emb, 'tp', 0, 0, tiled=True)  9.93 us
    all_to_all x2, starting transfers between devices, spread(): return jnp.sum(lax.all_to_all(copies, axis, 0, 0, tiled=True), axis=0)  9.01 us
  transfers between devices with their start and end apart: 3, of which 3 were waited for; matrix products, arithmetic and copies ran while one was open for 0% of the time, Pallas kernels for 0%

profile of v4, /device:TPU:8, one launch (start us, length us, event | category | flops | bytes accessed | tf_op | source)
XLA Modules:
  0.0 160.1 jit_solution(3454870478779399237)
XLA Ops:
  0.7 1.3 copy.55
  2.0 0.7 concatenate.17
  2.7 0.3 concatenate.18
  3.0 1.3 pad_maximum_fusion
  4.3 0.1 copy.56
  4.4 4.5 %all_to_all.38 = bf16[64,2,3840]{2,0,1:T(8,128)(2,1)S(1)} all-to-all(bf16[64,2,3840]{2,0,1:T(8,128)(2,1)S(1)} %copy.56), channel_id=1, replica_groups=mesh['z'=8,'y'=8,'c'=2,'tp'=4] {'c'}, dimensions={1} | all-to-all | bytes 1966080 | tf_op jit(solution)/shard_map/all_to_all | solution.py:64
  8.9 0.1 convert_reduce_fusion
  9.1 1.6 %all_to_all.26 = f32[64,1,3840]{2,1,0:T(1,128)} reshape(f32[64,3840]{1,0:T(8,128)S(1)} %convert_reduce_fusion) | data formatting | bytes 1966080 | tf_op jit(solution)/shard_map/all_to_all | solution.py:68
  10.7 16.7 %all-to-all-start.1 = ((f32[64,1,3840]{2,1,0:T(1,128)}), f32[64,1,3840]{2,1,0:T(1,128)S(1)}, u32[]{:S(2)}, u32[]{:S(2)}) async-start(f32[64,1,3840]{2,1,0:T(1,128)} %all_to_all.26), calls=%async_computation.1 | async-start | bytes 1966080 | tf_op jit(solution)/shard_map/all_to_all | solution.py:68
  27.5 0.6 multiply_reduce_fusion
  28.1 27.5 %all-to-all-done.1 = f32[64,1,3840]{2,1,0:T(1,128)S(1)} async-done(((f32[64,1,3840]{2,1,0:T(1,128)}), f32[64,1,3840]{2,1,0:T(1,128)S(1)}, u32[]{:S(2)}, u32[]{:S(2)}) %all-to-all-start.1) | async-done | bytes 983072 | tf_op jit(solution)/shard_map/all_to_all | solution.py:68
  55.6 0.6 reduce_sum.73
  56.2 0.0 copy-start.7
  56.2 0.0 copy-start.8
  56.2 0.6 multiply_reduce_fusion.1
  58.1 0.1 pad_maximum_fusion.3
  58.2 0.7 broadcast_in_dim.9
  58.9 5.7 %all-to-all-start.2 = ((f32[16,1,1345]{2,1,0:T(1,128)}), f32[16,1,1345]{2,1,0:T(1,128)S(1)}, u32[]{:S(2)}, u32[]{:S(2)}) async-start(f32[16,1,1345]{2,1,0:T(1,128)} %broadcast_in_dim.9), calls=%async_computation.2 | async-start | bytes 180224 | tf_op jit(solution)/shard_map/all_to_all | solution.py:77
  64.5 0.1 reshape.124
  64.7 6.6 %all-to-all-done.2 = f32[16,1,1345]{2,1,0:T(1,128)S(1)} async-done(((f32[16,1,1345]{2,1,0:T(1,128)}), f32[16,1,1345]{2,1,0:T(1,128)S(1)}, u32[]{:S(2)}, u32[]{:S(2)}) %all-to-all-start.2) | async-done | bytes 86112 | tf_op jit(solution)/shard_map/all_to_all | solution.py:77
  71.2 0.1 reduce_sum.76
  71.3 0.1 pad_maximum_fusion.1
  71.4 0.1 all_to_all.29
  71.5 9.9 %all_to_all.39 = f32[4,1,6465]{2,1,0:T(1,128)S(1)} all-to-all(f32[4,1,6465]{2,1,0:T(1,128)S(1)} %all_to_all.29), channel_id=1, replica_groups=mesh['z'=8,'y'=8,'c'=2,'tp'=4] {'tp'}, dimensions={0} | all-to-all | bytes 206880 | tf_op jit(solution)/shard_map/all_to_all | solution.py:84
  81.5 0.6 broadcast_in_dim.11
  82.1 3.3 %all-to-all-start.4 = ((f32[8,1,1345]{2,1,0:T(1,128)}), f32[8,1,1345]{2,1,0:T(1,128)S(1)}, u32[]{:S(2)}, u32[]{:S(2)}) async-start(f32[8,1,1345]{2,1,0:T(1,128)} %broadcast_in_dim.11), calls=%async_computation.4 | async-start | bytes 90112 | tf_op jit(solution)/shard_map/all_to_all | solution.py:77
  86.2 7.3 %all-to-all-done.4 = f32[8,1,1345]{2,1,0:T(1,128)S(1)} async-done(((f32[8,1,1345]{2,1,0:T(1,128)}), f32[8,1,1345]{2,1,0:T(1,128)S(1)}, u32[]{:S(2)}, u32[]{:S(2)}) %all-to-all-start.4) | async-done | bytes 43072 | tf_op jit(solution)/shard_map/all_to_all | solution.py:77
  93.6 0.5 slice.41
  94.1 0.7 multiply_reduce_fusion.2
  96.2 0.1 slice_multiply_fusion
  96.3 0.7 convert_bitcast_fusion
  97.0 16.4 %all-gather.2 = bf16[16,1,3840]{2,1,0:T(2,128)(2,1)S(1)} all-gather(bf16[1,1,3840]{2,1,0:T(2,128)(2,1)S(1)} %get-tuple-element.102), channel_id=1, replica_groups=mesh['z'=8,'y'=8,'c'=2,'tp'=4] {'y','c'}, dimensions={0}, use_global_device_ids=true | all-gather | bytes 130560 | tf_op jit(solution)/shard_map/all_gather | solution.py:116
  113.4 26.6 %all-gather = bf16[128,3840]{1,0:T(8,128)(2,1)S(1)} all-gather(bf16[16,3840]{1,0:T(8,128)(2,1)S(1)} %bitcast.19), channel_id=2, replica_groups=mesh['z'=8,'y'=8,'c'=2,'tp'=4] {'z'}, dimensions={0}, use_global_device_ids=true | all-gather | bytes 1105920 | tf_op jit(solution)/shard_map/all_gather | solution.py:117
  140.0 0.1 fusion.7
  140.1 0.8 reshape.125
  140.9 0.0 copy-start.3
  140.9 0.0 copy-start.4
  140.9 0.0 copy-start.5
  141.0 0.1 reshape.127
  141.1 0.2 reshape.126
  141.3 0.0 copy-start
  141.3 0.1 constant_dynamic-slice_fusion.1
  141.4 0.1 reshape.128
  141.6 0.1 mul.227
  141.7 0.1 mul.229
  141.8 0.0 copy-done.4
  141.8 0.0 copy-done.5
  141.9 0.8 fusion.3
  142.6 0.1 reshape.129
  142.7 0.1 reshape.142
  142.8 12.5 %all-gather.3 = bf16[4,1,24320]{2,1,0:T(2,128)(2,1)S(1)} all-gather(bf16[1,1,24320]{2,1,0:T(2,128)(2,1)S(1)} %reshape.142), channel_id=3, replica_groups=mesh['z'=8,'y'=8,'c'=2,'tp'=4] {'tp'}, dimensions={0}, use_global_device_ids=true | all-gather | bytes 243200 | tf_op jit(solution)/shard_map/all_gather | solution.py:126
  155.3 0.1 copy.73
  155.4 0.1 slice.48
  155.5 0.0 copy-start.9
  155.5 0.0 copy-start.10
  155.5 0.0 copy-start.11
  155.6 1.0 copy.61
  156.6 0.1 reshape.133
  156.7 0.4 reshape.132
  157.1 0.7 copy.62
  157.8 0.1 reshape.130
  157.9 0.7 reshape.131
  158.6 0.7 constant_dynamic-slice_fusion
  159.4 0.7 multiply_subtract_fusion.2
  (27 shorter events, 0.3 us)
Async XLA Ops:
  0.6 2.1 %copy-start.1 = (bf16[1,192,1280]{2,1,0:T(8,128)(2,1)S(1)}, bf16[1,192,1280]{2,1,0:T(8,128)(2,1)}, u32[]{:S(2)}) copy-start(bf16[1,192,1280]{2,1,0:T(8,128)(2,1)} %param.15) | copy-start | bytes 1474564
  10.7 16.7 %copy-start.12 = (f32[1,1,1344]{2,1,0:T(1,128)S(1)}, f32[1,1,1344]{2,1,0:T(1,128)}, u32[]{:S(2)}) copy-start(f32[1,1,1344]{2,1,0:T(1,128)} %param.16) | copy-start | bytes 16132
  10.7 16.8 %copy-start.2 = (bf16[64,320]{1,0:T(8,128)(2,1)S(1)}, bf16[64,320]{1,0:T(8,128)(2,1)}, u32[]{:S(2)}) copy-start(bf16[64,320]{1,0:T(8,128)(2,1)} %param.17) | copy-start | bytes 122884
  10.7 44.9 %all-to-all-start.1 = ((f32[64,1,3840]{2,1,0:T(1,128)}), f32[64,1,3840]{2,1,0:T(1,128)S(1)}, u32[]{:S(2)}, u32[]{:S(2)}) async-start(f32[64,1,3840]{2,1,0:T(1,128)} %all_to_all.26), calls=%async_computation.1 | async-start | bytes 1966080 | tf_op jit(solution)/shard_map/all_to_all | solution.py:68
  56.2 40.1 %copy-start.6 = (f32[1,3840]{1,0:T(1,128)S(1)}, f32[1,3840]{1,0:T(1,128)}, u32[]{:S(2)}) copy-start(f32[1,3840]{1,0:T(1,128)} %param.18) | copy-start | bytes 46084
  56.2 40.1 %copy-start.7 = (f32[1,3840]{1,0:T(1,128)S(1)}, f32[1,3840]{1,0:T(1,128)}, u32[]{:S(2)}) copy-start(f32[1,3840]{1,0:T(1,128)} %param.20) | copy-start | bytes 46084
  56.2 40.1 %copy-start.8 = (f32[1,3840]{1,0:T(1,128)S(1)}, f32[1,3840]{1,0:T(1,128)}, u32[]{:S(2)}) copy-start(f32[1,3840]{1,0:T(1,128)} %param.19) | copy-start | bytes 46084
  58.9 12.3 %all-to-all-start.2 = ((f32[16,1,1345]{2,1,0:T(1,128)}), f32[16,1,1345]{2,1,0:T(1,128)S(1)}, u32[]{:S(2)}, u32[]{:S(2)}) async-start(f32[16,1,1345]{2,1,0:T(1,128)} %broadcast_in_dim.9), calls=%async_computation.2 | async-start | bytes 180224 | tf_op jit(solution)/shard_map/all_to_all | solution.py:77
  82.1 11.4 %all-to-all-start.4 = ((f32[8,1,1345]{2,1,0:T(1,128)}), f32[8,1,1345]{2,1,0:T(1,128)S(1)}, u32[]{:S(2)}, u32[]{:S(2)}) async-start(f32[8,1,1345]{2,1,0:T(1,128)} %broadcast_in_dim.11), calls=%async_computation.4 | async-start | bytes 90112 | tf_op jit(solution)/shard_map/all_to_all | solution.py:77
  140.9 0.9 copy-start.3
  140.9 0.9 copy-start.4
  140.9 0.9 copy-start.5
  141.3 14.0 %copy-start = (bf16[192,1280]{1,0:T(8,128)(2,1)}, bf16[192,1280]{1,0:T(8,128)(2,1)S(1)}, u32[]{:S(2)}) copy-start(bf16[192,1280]{1,0:T(8,128)(2,1)S(1)} %reshape.126) | copy-start | bytes 1474564
  155.5 3.8 %copy-start.9 = (f32[1344]{0:T(1024)S(1)}, f32[1344]{0:T(1024)}, u32[]{:S(2)}) copy-start(f32[1344]{0:T(1024)} %param.24) | copy-start | bytes 16132
  155.5 3.8 %copy-start.10 = (f32[1344]{0:T(1024)S(1)}, f32[1344]{0:T(1024)}, u32[]{:S(2)}) copy-start(f32[1344]{0:T(1024)} %param.26) | copy-start | bytes 16132
  155.5 3.8 %copy-start.11 = (f32[1344]{0:T(1024)S(1)}, f32[1344]{0:T(1024)}, u32[]{:S(2)}) copy-start(f32[1344]{0:T(1024)} %param.25) | copy-start | bytes 16132

commit v5 on v3

--- a/solution.py
+++ b/solution.py
@@ -67,8 +67,19 @@
     partial = jnp.sum(halves.astype(jnp.float32), axis=1)
     pieces = lax.all_to_all(partial, ("z", "y"), 0, 0, tiled=True)
     grad_piece = jnp.sum(pieces, axis=0)
-    emb_piece = lax.all_to_all(emb_grad, "tp", split_axis=0, concat_axis=1, tiled=True).astype(
-        jnp.float32
+    tp_index = lax.axis_index("tp")
+    emb_chunks = emb_grad.reshape(tp_count, emb_grad.shape[0] // tp_count, emb_grad.shape[1])
+    by_shift = [emb_chunks[tp_index]]
+    for shift in range(1, tp_count):
+        outgoing = emb_chunks[(tp_index + shift) % tp_count]
+        pairs = [(i, (i + shift) % tp_count) for i in range(tp_count)]
+        by_shift.append(lax.ppermute(outgoing, "tp", pairs))
+    by_shift = jnp.stack(by_shift)
+    by_source = by_shift[(tp_index - jnp.arange(tp_count)) % tp_count]
+    emb_piece = (
+        by_source.transpose(1, 0, 2)
+        .reshape(emb_chunks.shape[1], tp_count * emb_grad.shape[1])
+        .astype(jnp.float32)
     )
     emb_float = emb_grad.astype(jnp.float32)
     local_squares = jnp.sum(grad_piece * grad_piece) + jnp.sum(emb_float * emb_float)
@@ -110,7 +121,9 @@
     o_block = lax.dynamic_slice_in_dim(o_weight, block_start, block_rows, 1)
     emb_rows = emb_new.astype(jnp.bfloat16)
     payload = jnp.concatenate([q_block.reshape(-1), o_block.reshape(-1), emb_rows.reshape(-1)])
-    shared = lax.all_gather(payload, "tp", axis=0, tiled=False)
+    shared = lax.all_to_all(
+        jnp.broadcast_to(payload[None], (tp_count,) + payload.shape), "tp", 0, 0, tiled=True
+    )
     q_len = block_rows * q_columns
     q_average = (
         shared[:, :q_len]
@@ -121,7 +134,7 @@
     o_average = shared[:, q_len : 2 * q_len].reshape(tp_count * q_columns, block_rows)
     emb_all = shared[:, 2 * q_len :].reshape(tp_count * emb_new.shape[0], width)
     emb_cols = width // tp_count
-    emb_weight = lax.dynamic_slice_in_dim(emb_all, lax.axis_index("tp") * emb_cols, emb_cols, 1)
+    emb_weight = lax.dynamic_slice_in_dim(emb_all, tp_index * emb_cols, emb_cols, 1)
     return (
         flat_new[None, :],
         flat_one[None, :],

time: 160 us -> 159 us (level)
  the two profiles are of different devices: /device:TPU:8 before, /device:TPU:2 now
where the time goes in v5:
time: 159 us; the launch traced here: 158 us
  blocking collectives  48.9 us (31%)
  starting transfers between devices  43 us (27%)
  waiting for transfers between devices  39.8 us (25%)
  local copies, waits for them, and re-layouts  13.9 us (9%)
  other arithmetic  8.25 us (5%)
  between operations  4.54 us (3%)
    all_to_all x1, waiting for transfers between devices, body(): pieces = lax.all_to_all(partial, ('z', 'y'), 0, 0, tiled=True)  27.8 us
    all_gather x1, blocking collectives, body(): gathered = lax.all_gather(gathered, 'z', axis=0, tiled=False).reshape(-1)  26.7 us
    all_gather x1, blocking collectives, body(): lax.all_gather(flat_new.astype(jnp.bfloat16), ('y', 'c'), axis=0, tiled=F...  17.7 us
    all_to_all x1, starting transfers between devices, body(): pieces = lax.all_to_all(partial, ('z', 'y'), 0, 0, tiled=True)  16.7 us
    ppermute x3, starting transfers between devices, body(): by_shift.append(lax.ppermute(outgoing, 'tp', pairs))  11.2 us
    all_to_all x2, starting transfers between devices, body(): packed = jnp.sum(lax.all_to_all(copies, axis, 0, 0, tiled=True), axis=0)  9.63 us
    all_to_all x2, waiting for transfers between devices, body(): packed = jnp.sum(lax.all_to_all(copies, axis, 0, 0, tiled=True), axis=0)  7.84 us
    all_to_all x1, starting transfers between devices, body(): lax.all_to_all(jnp.broadcast_to(payload[None], (tp_count,) + payload.shap...  5.39 us
  transfers between devices with their start and end apart: 7, of which 3 were waited for; matrix products, arithmetic and copies ran while one was open for 2% of the time, Pallas kernels for 0%

profile of v5, /device:TPU:2, one launch (start us, length us, event | category | flops | bytes accessed | tf_op | source)
XLA Modules:
  0.0 158.4 jit_solution(2949711476217370968)
XLA Ops:
  0.7 1.3 copy.55
  2.0 0.7 concatenate.14
  2.7 0.3 concatenate.15
  3.0 1.3 pad_maximum_fusion
  4.3 0.1 copy.56
  4.4 4.5 %all_to_all.35 = bf16[64,2,3840]{2,0,1:T(8,128)(2,1)S(1)} all-to-all(bf16[64,2,3840]{2,0,1:T(8,128)(2,1)S(1)} %copy.56), channel_id=1, replica_groups=mesh['z'=8,'y'=8,'c'=2,'tp'=4] {'c'}, dimensions={1} | all-to-all | bytes 1966080 | tf_op jit(solution)/shard_map/all_to_all | solution.py:64
  8.9 0.1 convert_reduce_fusion
  9.1 1.6 %all_to_all.24 = f32[64,1,3840]{2,1,0:T(1,128)} reshape(f32[64,3840]{1,0:T(8,128)S(1)} %convert_reduce_fusion) | data formatting | bytes 1966080 | tf_op jit(solution)/shard_map/all_to_all | solution.py:68
  10.7 16.7 %all-to-all-start.1 = ((f32[64,1,3840]{2,1,0:T(1,128)}), f32[64,1,3840]{2,1,0:T(1,128)S(1)}, u32[]{:S(2)}, u32[]{:S(2)}) async-start(f32[64,1,3840]{2,1,0:T(1,128)} %all_to_all.24), calls=%async_computation.1 | async-start | bytes 1966080 | tf_op jit(solution)/shard_map/all_to_all | solution.py:68
  27.5 0.6 multiply_reduce_fusion
  28.1 27.8 %all-to-all-done.1 = f32[64,1,3840]{2,1,0:T(1,128)S(1)} async-done(((f32[64,1,3840]{2,1,0:T(1,128)}), f32[64,1,3840]{2,1,0:T(1,128)S(1)}, u32[]{:S(2)}, u32[]{:S(2)}) %all-to-all-start.1) | async-done | bytes 983072 | tf_op jit(solution)/shard_map/all_to_all | solution.py:68
  55.9 0.6 reduce_sum.64
  56.5 0.6 multiply_reduce_fusion.1
  58.4 0.1 pad_maximum_fusion.3
  58.5 0.7 broadcast_in_dim.9
  59.2 5.0 %all-to-all-start.2 = ((f32[16,1,1345]{2,1,0:T(1,128)}), f32[16,1,1345]{2,1,0:T(1,128)S(1)}, u32[]{:S(2)}, u32[]{:S(2)}) async-start(f32[16,1,1345]{2,1,0:T(1,128)} %broadcast_in_dim.9), calls=%async_computation.2 | async-start | bytes 180224 | tf_op jit(solution)/shard_map/all_to_all | solution.py:91
  64.2 0.0 copy-start.3
  64.2 0.0 copy-start.4
  64.2 0.0 copy-start.5
  64.3 2.6 %collective-permute-start.2 = (bf16[16,320]{1,0:T(8,128)(2,1)S(1)}, bf16[16,320]{1,0:T(8,128)(2,1)S(1)}, u32[]{:S(2)}, u32[]{:S(2)}) collective-permute-start(bf16[16,320]{1,0:T(8,128)(2,1)S(1)} %get-tuple-element.114), channel_id=1, source_target_pairs={{0,3},{1,0},{2,1},{3,2},{4,7},{5,4},{6,5},{7,6},{8,11},{9,8},{10,9... | collective-permute-start | bytes 30728 | tf_op jit(solution)/shard_map/ppermute | solution.py:76
  66.9 3.4 %collective-permute-start = (bf16[16,320]{1,0:T(8,128)(2,1)S(1)}, bf16[16,320]{1,0:T(8,128)(2,1)S(1)}, u32[]{:S(2)}, u32[]{:S(2)}) collective-permute-start(bf16[16,320]{1,0:T(8,128)(2,1)S(1)} %get-tuple-element.116), channel_id=1, source_target_pairs={{0,1},{1,2},{2,3},{3,0},{4,5},{5,6},{6,7},{7,4},{8,9},{9,10},{10,1... | collective-permute-start | bytes 30728 | tf_op jit(solution)/shard_map/ppermute | solution.py:76
  70.3 5.2 %collective-permute-start.1 = (bf16[16,320]{1,0:T(8,128)(2,1)S(1)}, bf16[16,320]{1,0:T(8,128)(2,1)S(1)}, u32[]{:S(2)}, u32[]{:S(2)}) collective-permute-start(bf16[16,320]{1,0:T(8,128)(2,1)S(1)} %get-tuple-element.115), channel_id=1, source_target_pairs={{0,2},{1,3},{2,0},{3,1},{4,6},{5,7},{6,4},{7,5},{8,10},{9,11},{10,... | collective-permute-start | bytes 30728 | tf_op jit(solution)/shard_map/ppermute | solution.py:76
  75.5 0.1 reduce_sum.67
  75.6 0.8 broadcast_in_dim.10
  76.4 4.6 %all-to-all-start.3 = ((f32[32,1,1345]{2,1,0:T(1,128)}), f32[32,1,1345]{2,1,0:T(1,128)S(1)}, u32[]{:S(2)}, u32[]{:S(2)}) async-start(f32[32,1,1345]{2,1,0:T(1,128)} %broadcast_in_dim.10), calls=%async_computation.3 | async-start | bytes 360448 | tf_op jit(solution)/shard_map/all_to_all | solution.py:91
  81.8 0.0 collective-permute-done.1
  81.9 0.6 gather_fusion
  82.4 7.8 %all-to-all-done.3 = f32[32,1,1345]{2,1,0:T(1,128)S(1)} async-done(((f32[32,1,1345]{2,1,0:T(1,128)}), f32[32,1,1345]{2,1,0:T(1,128)S(1)}, u32[]{:S(2)}, u32[]{:S(2)}) %all-to-all-start.3) | async-done | bytes 172192 | tf_op jit(solution)/shard_map/all_to_all | solution.py:91
  90.3 0.1 reduce_sum.68
  90.4 0.5 slice.34
  90.9 0.7 multiply_reduce_fusion.2
  93.0 0.1 mul.225
  93.2 0.7 fusion.5
  93.9 0.1 reshape.179
  94.0 0.7 convert_bitcast_fusion
  94.7 17.7 %all-gather.1 = bf16[16,1,3840]{2,1,0:T(2,128)(2,1)S(1)} all-gather(bf16[1,1,3840]{2,1,0:T(2,128)(2,1)S(1)} %get-tuple-element.102), channel_id=1, replica_groups=mesh['z'=8,'y'=8,'c'=2,'tp'=4] {'y','c'}, dimensions={0}, use_global_device_ids=true | all-gather | bytes 130560 | tf_op jit(solution)/shard_map/all_gather | solution.py:114
  112.4 26.7 %all-gather = bf16[128,3840]{1,0:T(8,128)(2,1)S(1)} all-gather(bf16[16,3840]{1,0:T(8,128)(2,1)S(1)} %bitcast.29), channel_id=2, replica_groups=mesh['z'=8,'y'=8,'c'=2,'tp'=4] {'z'}, dimensions={0}, use_global_device_ids=true | all-gather | bytes 1105920 | tf_op jit(solution)/shard_map/all_gather | solution.py:115
  139.2 0.1 fusion.9
  139.2 0.8 reshape.175
  140.0 1.0 copy.61
  141.0 0.1 reshape.177
  141.1 0.2 reshape.176
  141.4 0.0 copy-start
  141.4 0.1 constant_dynamic-slice_fusion.1
  141.5 0.0 copy-start.9
  141.5 0.0 copy-start.10
  141.5 0.0 copy-start.11
  141.5 0.1 reshape.178
  141.7 0.2 broadcast_in_dim.11
  141.9 0.5 broadcast.151
  142.4 1.9 %reduce.4 = bf16[4,24320]{1,0:T(4,128)(2,1)S(1)} reduce(bf16[4,1,24320]{2,1,0:T(2,128)(2,1)S(1)} %broadcast_in_dim.11, bf16[]{:T(256)} %broadcast.151), dimensions={1}, to_apply=%broadcast_in_dim.11.reduce_sub_computation | reduce | bytes 389122 | tf_op jit(solution)/shard_map/broadcast_in_dim | solution.py:125
  144.3 0.7 reshape.200
  145.0 5.4 %all-to-all-start.4 = ((bf16[4,2,12160]{2,1,0:T(2,128)(2,1)}), bf16[4,2,12160]{2,1,0:T(2,128)(2,1)S(1)}, u32[]{:S(2)}, u32[]{:S(2)}) async-start(bf16[4,2,12160]{2,1,0:T(2,128)(2,1)} %reshape.200), calls=%async_computation.4 | async-start | bytes 389120 | tf_op jit(solution)/shard_map/all_to_all | solution.py:124
  150.4 0.7 multiply_subtract_fusion.2
  151.1 4.2 %all-to-all-done.4 = bf16[4,2,12160]{2,1,0:T(2,128)(2,1)S(1)} async-done(((bf16[4,2,12160]{2,1,0:T(2,128)(2,1)}), bf16[4,2,12160]{2,1,0:T(2,128)(2,1)S(1)}, u32[]{:S(2)}, u32[]{:S(2)}) %all-to-all-start.4) | async-done | bytes 194592 | tf_op jit(solution)/shard_map/all_to_all | solution.py:124
  155.3 0.1 reshape.201
  155.4 0.1 copy.71
  155.5 0.1 slice.40
  155.6 0.1 reshape.183
  155.7 0.4 reshape.182
  156.1 0.7 copy.62
  156.9 0.1 reshape.180
  157.0 0.7 reshape.181
  157.7 0.7 constant_dynamic-slice_fusion
  (35 shorter events, 0.3 us)
Async XLA Ops:
  0.6 2.1 %copy-start.1 = (bf16[1,192,1280]{2,1,0:T(8,128)(2,1)S(1)}, bf16[1,192,1280]{2,1,0:T(8,128)(2,1)}, u32[]{:S(2)}) copy-start(bf16[1,192,1280]{2,1,0:T(8,128)(2,1)} %param.15) | copy-start | bytes 1474564
  10.7 16.7 %copy-start.12 = (f32[1,1,1344]{2,1,0:T(1,128)S(1)}, f32[1,1,1344]{2,1,0:T(1,128)}, u32[]{:S(2)}) copy-start(f32[1,1,1344]{2,1,0:T(1,128)} %param.16) | copy-start | bytes 16132
  10.7 16.8 %copy-start.2 = (bf16[64,320]{1,0:T(8,128)(2,1)S(1)}, bf16[64,320]{1,0:T(8,128)(2,1)}, u32[]{:S(2)}) copy-start(bf16[64,320]{1,0:T(8,128)(2,1)} %param.17) | copy-start | bytes 122884
  10.7 45.2 %all-to-all-start.1 = ((f32[64,1,3840]{2,1,0:T(1,128)}), f32[64,1,3840]{2,1,0:T(1,128)S(1)}, u32[]{:S(2)}, u32[]{:S(2)}) async-start(f32[64,1,3840]{2,1,0:T(1,128)} %all_to_all.24), calls=%async_computation.1 | async-start | bytes 1966080 | tf_op jit(solution)/shard_map/all_to_all | solution.py:68
  59.2 16.3 %all-to-all-start.2 = ((f32[16,1,1345]{2,1,0:T(1,128)}), f32[16,1,1345]{2,1,0:T(1,128)S(1)}, u32[]{:S(2)}, u32[]{:S(2)}) async-start(f32[16,1,1345]{2,1,0:T(1,128)} %broadcast_in_dim.9), calls=%async_computation.2 | async-start | bytes 180224 | tf_op jit(solution)/shard_map/all_to_all | solution.py:91
  64.2 29.0 %copy-start.3 = (f32[16,1280]{1,0:T(8,128)S(1)}, f32[16,1280]{1,0:T(8,128)}, u32[]{:S(2)}) copy-start(f32[16,1280]{1,0:T(8,128)} %param.21) | copy-start | bytes 245764
  64.2 29.0 %copy-start.4 = (f32[16,1280]{1,0:T(8,128)S(1)}, f32[16,1280]{1,0:T(8,128)}, u32[]{:S(2)}) copy-start(f32[16,1280]{1,0:T(8,128)} %param.23) | copy-start | bytes 245764
  64.2 29.0 %copy-start.5 = (f32[16,1280]{1,0:T(8,128)S(1)}, f32[16,1280]{1,0:T(8,128)}, u32[]{:S(2)}) copy-start(f32[16,1280]{1,0:T(8,128)} %param.22) | copy-start | bytes 245764
  64.3 17.5 %collective-permute-start.2 = (bf16[16,320]{1,0:T(8,128)(2,1)S(1)}, bf16[16,320]{1,0:T(8,128)(2,1)S(1)}, u32[]{:S(2)}, u32[]{:S(2)}) collective-permute-start(bf16[16,320]{1,0:T(8,128)(2,1)S(1)} %get-tuple-element.114), channel_id=1, source_target_pairs={{0,3},{1,0},{2,1},{3,2},{4,7},{5,4},{6,5},{7,6},{8,11},{9,8},{10,9... | collective-permute-start | bytes 30728 | tf_op jit(solution)/shard_map/ppermute | solution.py:76
  66.9 15.0 %collective-permute-start = (bf16[16,320]{1,0:T(8,128)(2,1)S(1)}, bf16[16,320]{1,0:T(8,128)(2,1)S(1)}, u32[]{:S(2)}, u32[]{:S(2)}) collective-permute-start(bf16[16,320]{1,0:T(8,128)(2,1)S(1)} %get-tuple-element.116), channel_id=1, source_target_pairs={{0,1},{1,2},{2,3},{3,0},{4,5},{5,6},{6,7},{7,4},{8,9},{9,10},{10,1... | collective-permute-start | bytes 30728 | tf_op jit(solution)/shard_map/ppermute | solution.py:76
  70.3 11.6 %collective-permute-start.1 = (bf16[16,320]{1,0:T(8,128)(2,1)S(1)}, bf16[16,320]{1,0:T(8,128)(2,1)S(1)}, u32[]{:S(2)}, u32[]{:S(2)}) collective-permute-start(bf16[16,320]{1,0:T(8,128)(2,1)S(1)} %get-tuple-element.115), channel_id=1, source_target_pairs={{0,2},{1,3},{2,0},{3,1},{4,6},{5,7},{6,4},{7,5},{8,10},{9,11},{10,... | collective-permute-start | bytes 30728 | tf_op jit(solution)/shard_map/ppermute | solution.py:76
  76.4 17.6 %copy-start.6 = (f32[1,3840]{1,0:T(1,128)S(1)}, f32[1,3840]{1,0:T(1,128)}, u32[]{:S(2)}) copy-start(f32[1,3840]{1,0:T(1,128)} %param.18) | copy-start | bytes 46084
  76.4 17.6 %copy-start.7 = (f32[1,3840]{1,0:T(1,128)S(1)}, f32[1,3840]{1,0:T(1,128)}, u32[]{:S(2)}) copy-start(f32[1,3840]{1,0:T(1,128)} %param.20) | copy-start | bytes 46084
  76.4 17.6 %copy-start.8 = (f32[1,3840]{1,0:T(1,128)S(1)}, f32[1,3840]{1,0:T(1,128)}, u32[]{:S(2)}) copy-start(f32[1,3840]{1,0:T(1,128)} %param.19) | copy-start | bytes 46084
  76.4 13.9 %all-to-all-start.3 = ((f32[32,1,1345]{2,1,0:T(1,128)}), f32[32,1,1345]{2,1,0:T(1,128)S(1)}, u32[]{:S(2)}, u32[]{:S(2)}) async-start(f32[32,1,1345]{2,1,0:T(1,128)} %broadcast_in_dim.10), calls=%async_computation.3 | async-start | bytes 360448 | tf_op jit(solution)/shard_map/all_to_all | solution.py:91
  141.4 3.7 %copy-start = (bf16[192,1280]{1,0:T(8,128)(2,1)}, bf16[192,1280]{1,0:T(8,128)(2,1)S(1)}, u32[]{:S(2)}) copy-start(bf16[192,1280]{1,0:T(8,128)(2,1)S(1)} %reshape.176) | copy-start | bytes 1474564
  141.5 9.0 %copy-start.9 = (f32[1344]{0:T(1024)S(1)}, f32[1344]{0:T(1024)}, u32[]{:S(2)}) copy-start(f32[1344]{0:T(1024)} %param.24) | copy-start | bytes 16132
  141.5 8.9 %copy-start.10 = (f32[1344]{0:T(1024)S(1)}, f32[1344]{0:T(1024)}, u32[]{:S(2)}) copy-start(f32[1344]{0:T(1024)} %param.26) | copy-start | bytes 16132
  141.5 8.9 %copy-start.11 = (f32[1344]{0:T(1024)S(1)}, f32[1344]{0:T(1024)}, u32[]{:S(2)}) copy-start(f32[1344]{0:T(1024)} %param.25) | copy-start | bytes 16132
  145.0 10.3 %all-to-all-start.4 = ((bf16[4,2,12160]{2,1,0:T(2,128)(2,1)}), bf16[4,2,12160]{2,1,0:T(2,128)(2,1)S(1)}, u32[]{:S(2)}, u32[]{:S(2)}) async-start(bf16[4,2,12160]{2,1,0:T(2,128)(2,1)} %reshape.200), calls=%async_computation.4 | async-start | bytes 389120 | tf_op jit(solution)/shard_map/all_to_all | solution.py:124

commit v6 on v3

--- a/solution.py
+++ b/solution.py
@@ -67,8 +67,15 @@
     partial = jnp.sum(halves.astype(jnp.float32), axis=1)
     pieces = lax.all_to_all(partial, ("z", "y"), 0, 0, tiled=True)
     grad_piece = jnp.sum(pieces, axis=0)
-    emb_piece = lax.all_to_all(emb_grad, "tp", split_axis=0, concat_axis=1, tiled=True).astype(
-        jnp.float32
+    emb_blocks = lax.all_gather(emb_grad, "tp", axis=0, tiled=False)
+    emb_rows_count = emb_grad.shape[0] // tp_count
+    emb_mine = lax.dynamic_slice_in_dim(
+        emb_blocks, lax.axis_index("tp") * emb_rows_count, emb_rows_count, 1
+    )
+    emb_piece = (
+        emb_mine.transpose(1, 0, 2)
+        .reshape(emb_rows_count, tp_count * emb_grad.shape[1])
+        .astype(jnp.float32)
     )
     emb_float = emb_grad.astype(jnp.float32)
     local_squares = jnp.sum(grad_piece * grad_piece) + jnp.sum(emb_float * emb_float)

time: 160 us -> 158 us (0.988)
  blocking collectives: 73 us -> 86 us
  waiting for transfers between devices: 37.9 us -> 27.5 us
  starting transfers between devices: 25.5 us -> 22.2 us
    all_gather x0 -> x1, blocking collectives: none -> 12.9 us  [body(): emb_blocks = lax.all_gather(emb_grad, 'tp', axis=0, tiled=False)]
    all_to_all x1, waiting for transfers between devices: 11.2 us -> 0.01 us  [body(): packed = jnp.sum(lax.all_to_all(copies, axis, 0, 0, tiled=True), axis=0)]
    all_to_all x1 -> x0, starting transfers between devices: 3.28 us -> none  [body(): lax.all_to_all(emb_grad, 'tp', split_axis=0, concat_axis=1, tiled=True)]
    unnamed x30 -> x33, local copies, waits for them, and re-layouts: 3.41 us -> 3.47 us
  transfers between devices with their start and end apart: 3 -> 2, of which waited for: 2 -> 1; matrix products, arithmetic and copies ran while one was open for 3% -> 0% of each run, Pallas kernels for 0% -> 0%
where the time goes in v6:
time: 158 us
  blocking collectives  86 us (54%)
  waiting for transfers between devices  27.5 us (17%)
  starting transfers between devices  22.2 us (14%)
  local copies, waits for them, and re-layouts  11.2 us (7%)
  other arithmetic  6.39 us (4%)
  between operations  4.39 us (3%)
    all_to_all x1, waiting for transfers between devices, body(): pieces = lax.all_to_all(partial, ('z', 'y'), 0, 0, tiled=True)  27.5 us
    all_gather x1, blocking collectives, body(): gathered = lax.all_gather(gathered, 'z', axis=0, tiled=False).reshape(-1)  27.4 us
    all_to_all x1, starting transfers between devices, body(): pieces = lax.all_to_all(partial, ('z', 'y'), 0, 0, tiled=True)  16.7 us
    all_gather x1, blocking collectives, body(): lax.all_gather(flat_new.astype(jnp.bfloat16), ('y', 'c'), axis=0, tiled=F...  16.5 us
    all_gather x1, blocking collectives, body(): emb_blocks = lax.all_gather(emb_grad, 'tp', axis=0, tiled=False)  12.9 us
    all_gather x1, blocking collectives, body(): shared = lax.all_gather(payload, 'tp', axis=0, tiled=False)  12.5 us
    all_to_all x1, blocking collectives, body(): packed = jnp.sum(lax.all_to_all(copies, axis, 0, 0, tiled=True), axis=0)  12.1 us
    all_to_all x1, starting transfers between devices, body(): packed = jnp.sum(lax.all_to_all(copies, axis, 0, 0, tiled=True), axis=0)  5.48 us
  transfers between devices with their start and end apart: 2, of which 1 were waited for; matrix products, arithmetic and copies ran while one was open for 0% of the time, Pallas kernels for 0%

profile of v6, /device:TPU:8, one launch (start us, length us, event | category | flops | bytes accessed | tf_op | source)
XLA Modules:
  0.0 157.7 jit_solution(5339713355190256032)
XLA Ops:
  0.6 0.0 copy-start.1
  0.7 1.3 copy.57
  2.0 0.7 concatenate.14
  2.7 0.3 concatenate.15
  3.0 1.3 pad_maximum_fusion
  4.3 0.1 copy.58
  4.4 4.5 %all_to_all.26 = bf16[64,2,3840]{2,0,1:T(8,128)(2,1)S(1)} all-to-all(bf16[64,2,3840]{2,0,1:T(8,128)(2,1)S(1)} %copy.58), channel_id=1, replica_groups=mesh['z'=8,'y'=8,'c'=2,'tp'=4] {'c'}, dimensions={1} | all-to-all | bytes 1966080 | tf_op jit(solution)/shard_map/all_to_all | solution.py:64
  8.9 0.1 convert_reduce_fusion
  9.1 1.6 %all_to_all.18 = f32[64,1,3840]{2,1,0:T(1,128)} reshape(f32[64,3840]{1,0:T(8,128)S(1)} %convert_reduce_fusion) | data formatting | bytes 1966080 | tf_op jit(solution)/shard_map/all_to_all | solution.py:68
  10.7 16.7 %all-to-all-start.1 = ((f32[64,1,3840]{2,1,0:T(1,128)}), f32[64,1,3840]{2,1,0:T(1,128)S(1)}, u32[]{:S(2)}, u32[]{:S(2)}) async-start(f32[64,1,3840]{2,1,0:T(1,128)} %all_to_all.18), calls=%async_computation.1 | async-start | bytes 1966080 | tf_op jit(solution)/shard_map/all_to_all | solution.py:68
  27.4 0.0 copy-done.2
  27.5 0.6 multiply_reduce_fusion
  28.1 27.5 %all-to-all-done.1 = f32[64,1,3840]{2,1,0:T(1,128)S(1)} async-done(((f32[64,1,3840]{2,1,0:T(1,128)}), f32[64,1,3840]{2,1,0:T(1,128)S(1)}, u32[]{:S(2)}, u32[]{:S(2)}) %all-to-all-start.1) | async-done | bytes 983072 | tf_op jit(solution)/shard_map/all_to_all | solution.py:68
  55.6 0.6 reduce_sum.64
  56.2 0.0 copy-start.7
  56.2 0.0 copy-start.8
  56.2 0.6 multiply_reduce_fusion.1
  58.1 0.1 pad_maximum_fusion.2
  58.2 0.1 broadcast_in_dim.7
  58.2 12.1 %all_to_all.27 = f32[16,1,1345]{2,1,0:T(1,128)S(1)} all-to-all(f32[16,1,1345]{2,1,0:T(1,128)S(1)} %broadcast_in_dim.7), channel_id=1, replica_groups=mesh['z'=8,'y'=8,'c'=2,'tp'=4] {'y','c'}, dimensions={0} | all-to-all | bytes 172160 | tf_op jit(solution)/shard_map/all_to_all | solution.py:87
  70.4 0.1 reduce_sum.67
  70.5 0.8 broadcast_in_dim.8
  71.2 5.5 %all-to-all-start.3 = ((f32[32,1,1345]{2,1,0:T(1,128)}), f32[32,1,1345]{2,1,0:T(1,128)S(1)}, u32[]{:S(2)}, u32[]{:S(2)}) async-start(f32[32,1,1345]{2,1,0:T(1,128)} %broadcast_in_dim.8), calls=%async_computation.3 | async-start | bytes 360448 | tf_op jit(solution)/shard_map/all_to_all | solution.py:87
  77.4 12.9 %all-gather = bf16[256,320]{1,0:T(8,128)(2,1)S(1)} all-gather(bf16[64,320]{1,0:T(8,128)(2,1)S(1)} %copy-done.2), channel_id=2, replica_groups=mesh['z'=8,'y'=8,'c'=2,'tp'=4] {'tp'}, dimensions={0}, use_global_device_ids=true | all-gather | bytes 204800 | tf_op jit(solution)/shard_map/all_gather | solution.py:70
  90.3 0.0 all-to-all-done.3
  90.3 0.1 reduce_sum.68
  90.5 0.5 slice.32
  91.0 0.7 multiply_reduce_fusion.2
  93.1 0.7 convert_bitcast_fusion
  93.8 16.5 %all-gather.3 = bf16[16,1,3840]{2,1,0:T(2,128)(2,1)S(1)} all-gather(bf16[1,1,3840]{2,1,0:T(2,128)(2,1)S(1)} %get-tuple-element.102), channel_id=1, replica_groups=mesh['z'=8,'y'=8,'c'=2,'tp'=4] {'y','c'}, dimensions={0}, use_global_device_ids=true | all-gather | bytes 130560 | tf_op jit(solution)/shard_map/all_gather | solution.py:110
  110.3 27.4 %all-gather.1 = bf16[128,3840]{1,0:T(8,128)(2,1)S(1)} all-gather(bf16[16,3840]{1,0:T(8,128)(2,1)S(1)} %bitcast.19), channel_id=3, replica_groups=mesh['z'=8,'y'=8,'c'=2,'tp'=4] {'z'}, dimensions={0}, use_global_device_ids=true | all-gather | bytes 1105920 | tf_op jit(solution)/shard_map/all_gather | solution.py:111
  137.7 0.1 fusion.7
  137.8 0.8 reshape.116
  138.6 0.0 copy-start.3
  138.6 0.0 copy-start.4
  138.6 0.0 copy-start.5
  138.6 0.1 reshape.118
  138.7 0.2 reshape.117
  139.0 0.0 copy-start
  139.0 0.1 constant_dynamic-slice_fusion.1
  139.1 0.1 reshape.119
  139.3 0.1 mul.229
  139.4 0.0 copy-done.3
  139.5 0.0 copy-done.4
  139.5 0.0 copy-done.5
  139.6 0.8 fusion.3
  140.3 0.1 reshape.120
  140.4 0.1 reshape.134
  140.5 12.5 %all-gather.4 = bf16[4,1,24320]{2,1,0:T(2,128)(2,1)S(1)} all-gather(bf16[1,1,24320]{2,1,0:T(2,128)(2,1)S(1)} %reshape.134), channel_id=4, replica_groups=mesh['z'=8,'y'=8,'c'=2,'tp'=4] {'tp'}, dimensions={0}, use_global_device_ids=true | all-gather | bytes 243200 | tf_op jit(solution)/shard_map/all_gather | solution.py:120
  153.0 0.0 copy-done
  153.0 0.1 copy.76
  153.1 0.1 slice.38
  153.2 0.0 copy-start.9
  153.2 0.0 copy-start.10
  153.2 0.0 copy-start.11
  153.2 1.0 copy.63
  154.2 0.1 reshape.124
  154.3 0.4 reshape.123
  154.8 0.7 copy.64
  155.5 0.1 reshape.121
  155.6 0.7 reshape.122
  156.3 0.7 constant_dynamic-slice_fusion
  157.0 0.0 copy-done.9
  157.0 0.7 multiply_subtract_fusion.2
  (19 shorter events, 0.2 us)
Async XLA Ops:
  0.6 2.1 %copy-start.1 = (bf16[1,192,1280]{2,1,0:T(8,128)(2,1)S(1)}, bf16[1,192,1280]{2,1,0:T(8,128)(2,1)}, u32[]{:S(2)}) copy-start(bf16[1,192,1280]{2,1,0:T(8,128)(2,1)} %param.15) | copy-start | bytes 1474564
  10.7 16.7 %copy-start.12 = (f32[1,1,1344]{2,1,0:T(1,128)S(1)}, f32[1,1,1344]{2,1,0:T(1,128)}, u32[]{:S(2)}) copy-start(f32[1,1,1344]{2,1,0:T(1,128)} %param.16) | copy-start | bytes 16132
  10.7 16.8 %copy-start.2 = (bf16[64,320]{1,0:T(8,128)(2,1)S(1)}, bf16[64,320]{1,0:T(8,128)(2,1)}, u32[]{:S(2)}) copy-start(bf16[64,320]{1,0:T(8,128)(2,1)} %param.17) | copy-start | bytes 122884
  10.7 44.9 %all-to-all-start.1 = ((f32[64,1,3840]{2,1,0:T(1,128)}), f32[64,1,3840]{2,1,0:T(1,128)S(1)}, u32[]{:S(2)}, u32[]{:S(2)}) async-start(f32[64,1,3840]{2,1,0:T(1,128)} %all_to_all.18), calls=%async_computation.1 | async-start | bytes 1966080 | tf_op jit(solution)/shard_map/all_to_all | solution.py:68
  56.2 36.9 %copy-start.6 = (f32[1,3840]{1,0:T(1,128)S(1)}, f32[1,3840]{1,0:T(1,128)}, u32[]{:S(2)}) copy-start(f32[1,3840]{1,0:T(1,128)} %param.18) | copy-start | bytes 46084
  56.2 36.9 %copy-start.7 = (f32[1,3840]{1,0:T(1,128)S(1)}, f32[1,3840]{1,0:T(1,128)}, u32[]{:S(2)}) copy-start(f32[1,3840]{1,0:T(1,128)} %param.20) | copy-start | bytes 46084
  56.2 36.9 %copy-start.8 = (f32[1,3840]{1,0:T(1,128)S(1)}, f32[1,3840]{1,0:T(1,128)}, u32[]{:S(2)}) copy-start(f32[1,3840]{1,0:T(1,128)} %param.19) | copy-start | bytes 46084
  71.2 19.1 %all-to-all-start.3 = ((f32[32,1,1345]{2,1,0:T(1,128)}), f32[32,1,1345]{2,1,0:T(1,128)S(1)}, u32[]{:S(2)}, u32[]{:S(2)}) async-start(f32[32,1,1345]{2,1,0:T(1,128)} %broadcast_in_dim.8), calls=%async_computation.3 | async-start | bytes 360448 | tf_op jit(solution)/shard_map/all_to_all | solution.py:87
  138.6 0.9 copy-start.3
  138.6 0.9 copy-start.4
  138.6 0.9 copy-start.5
  139.0 14.0 %copy-start = (bf16[192,1280]{1,0:T(8,128)(2,1)}, bf16[192,1280]{1,0:T(8,128)(2,1)S(1)}, u32[]{:S(2)}) copy-start(bf16[192,1280]{1,0:T(8,128)(2,1)S(1)} %reshape.117) | copy-start | bytes 1474564
  153.2 3.8 %copy-start.9 = (f32[1344]{0:T(1024)S(1)}, f32[1344]{0:T(1024)}, u32[]{:S(2)}) copy-start(f32[1344]{0:T(1024)} %param.24) | copy-start | bytes 16132
  153.2 3.8 %copy-start.10 = (f32[1344]{0:T(1024)S(1)}, f32[1344]{0:T(1024)}, u32[]{:S(2)}) copy-start(f32[1344]{0:T(1024)} %param.26) | copy-start | bytes 16132
  153.2 3.8 %copy-start.11 = (f32[1344]{0:T(1024)S(1)}, f32[1344]{0:T(1024)}, u32[]{:S(2)}) copy-start(f32[1344]{0:T(1024)} %param.25) | copy-start | bytes 16132

commit v7 on v6

--- a/solution.py
+++ b/solution.py
@@ -77,8 +77,7 @@
         .reshape(emb_rows_count, tp_count * emb_grad.shape[1])
         .astype(jnp.float32)
     )
-    emb_float = emb_grad.astype(jnp.float32)
-    local_squares = jnp.sum(grad_piece * grad_piece) + jnp.sum(emb_float * emb_float)
+    local_squares = jnp.sum(grad_piece * grad_piece) + jnp.sum(emb_piece * emb_piece)
     gains_local = norm_grad[0, 0]
     packed = jnp.concatenate([local_squares[None], gains_local])
     for axis in (("y", "c"), ("z", "tp")):

time: 158 us -> 155 us (0.981)
    all_to_all x1, waiting for transfers between devices: 27.5 us -> 15 us  [body(): pieces = lax.all_to_all(partial, ('z', 'y'), 0, 0, tiled=True)]
    all_to_all x1, waiting for transfers between devices: 0.01 us -> 11.2 us  [body(): packed = jnp.sum(lax.all_to_all(copies, axis, 0, 0, tiled=True), axis=0)]
    unnamed x33 -> x32, local copies, waits for them, and re-layouts: 3.47 us -> 3.3 us
  transfers between devices with their start and end apart: 2 -> 2, of which waited for: 1 -> 2; matrix products, arithmetic and copies ran while one was open for 0% -> 0% of each run, Pallas kernels for 0% -> 0%
where the time goes in v7:
time: 155 us
  blocking collectives  84.7 us (55%)
  waiting for transfers between devices  26.2 us (17%)
  starting transfers between devices  22.2 us (14%)
  local copies, waits for them, and re-layouts  11.1 us (7%)
  other arithmetic  6.42 us (4%)
  between operations  4.4 us (3%)
    all_gather x1, blocking collectives, body(): gathered = lax.all_gather(gathered, 'z', axis=0, tiled=False).reshape(-1)  26.5 us
    all_to_all x1, starting transfers between devices, body(): pieces = lax.all_to_all(partial, ('z', 'y'), 0, 0, tiled=True)  16.7 us
    all_gather x1, blocking collectives, body(): lax.all_gather(flat_new.astype(jnp.bfloat16), ('y', 'c'), axis=0, tiled=F...  16.5 us
    all_to_all x1, waiting for transfers between devices, body(): pieces = lax.all_to_all(partial, ('z', 'y'), 0, 0, tiled=True)  15 us
    all_gather x1, blocking collectives, body(): shared = lax.all_gather(payload, 'tp', axis=0, tiled=False)  12.5 us
    all_gather x1, blocking collectives, body(): emb_blocks = lax.all_gather(emb_grad, 'tp', axis=0, tiled=False)  12.5 us
    all_to_all x1, blocking collectives, body(): packed = jnp.sum(lax.all_to_all(copies, axis, 0, 0, tiled=True), axis=0)  12.1 us
    all_to_all x1, waiting for transfers between devices, body(): packed = jnp.sum(lax.all_to_all(copies, axis, 0, 0, tiled=True), axis=0)  11.2 us
  transfers between devices with their start and end apart: 2, of which 2 were waited for; matrix products, arithmetic and copies ran while one was open for 0% of the time, Pallas kernels for 0%

profile of v7, /device:TPU:8, one launch (start us, length us, event | category | flops | bytes accessed | tf_op | source)
XLA Modules:
  0.0 155.0 jit_solution(15844735285191520301)
XLA Ops:
  0.6 0.0 copy-start.1
  0.7 1.3 copy.57
  2.0 0.7 concatenate.14
  2.7 0.0 copy-done.1
  2.7 0.3 concatenate.15
  3.0 1.3 pad_maximum_fusion
  4.3 0.1 copy.58
  4.4 4.5 %all_to_all.26 = bf16[64,2,3840]{2,0,1:T(8,128)(2,1)S(1)} all-to-all(bf16[64,2,3840]{2,0,1:T(8,128)(2,1)S(1)} %copy.58), channel_id=1, replica_groups=mesh['z'=8,'y'=8,'c'=2,'tp'=4] {'c'}, dimensions={1} | all-to-all | bytes 1966080 | tf_op jit(solution)/shard_map/all_to_all | solution.py:64
  8.9 0.1 convert_reduce_fusion
  9.1 1.6 %all_to_all.18 = f32[64,1,3840]{2,1,0:T(1,128)} reshape(f32[64,3840]{1,0:T(8,128)S(1)} %convert_reduce_fusion) | data formatting | bytes 1966080 | tf_op jit(solution)/shard_map/all_to_all | solution.py:68
  10.7 16.7 %all-to-all-start.1 = ((f32[64,1,3840]{2,1,0:T(1,128)}), f32[64,1,3840]{2,1,0:T(1,128)S(1)}, u32[]{:S(2)}, u32[]{:S(2)}) async-start(f32[64,1,3840]{2,1,0:T(1,128)} %all_to_all.18), calls=%async_computation.1 | async-start | bytes 1966080 | tf_op jit(solution)/shard_map/all_to_all | solution.py:68
  27.4 0.0 copy-done.12
  27.4 0.0 copy-done.5
  27.5 12.5 %all-gather = bf16[256,320]{1,0:T(8,128)(2,1)S(1)} all-gather(bf16[64,320]{1,0:T(8,128)(2,1)S(1)} %copy-done.5), channel_id=2, replica_groups=mesh['z'=8,'y'=8,'c'=2,'tp'=4] {'tp'}, dimensions={0}, use_global_device_ids=true | all-gather | bytes 204800 | tf_op jit(solution)/shard_map/all_gather | solution.py:70
  39.9 0.7 fusion
  40.6 15.0 %all-to-all-done.1 = f32[64,1,3840]{2,1,0:T(1,128)S(1)} async-done(((f32[64,1,3840]{2,1,0:T(1,128)}), f32[64,1,3840]{2,1,0:T(1,128)S(1)}, u32[]{:S(2)}, u32[]{:S(2)}) %all-to-all-start.1) | async-done | bytes 983072 | tf_op jit(solution)/shard_map/all_to_all | solution.py:68
  55.6 0.6 reduce_sum.64
  56.2 0.6 multiply_reduce_fusion
  58.1 0.1 pad_maximum_fusion.2
  58.2 0.1 broadcast_in_dim.7
  58.2 12.1 %all_to_all.27 = f32[16,1,1345]{2,1,0:T(1,128)S(1)} all-to-all(f32[16,1,1345]{2,1,0:T(1,128)S(1)} %broadcast_in_dim.7), channel_id=1, replica_groups=mesh['z'=8,'y'=8,'c'=2,'tp'=4] {'y','c'}, dimensions={0} | all-to-all | bytes 172160 | tf_op jit(solution)/shard_map/all_to_all | solution.py:86
  70.4 0.1 reduce_sum.67
  70.4 0.8 broadcast_in_dim.8
  71.2 5.5 %all-to-all-start.3 = ((f32[32,1,1345]{2,1,0:T(1,128)}), f32[32,1,1345]{2,1,0:T(1,128)S(1)}, u32[]{:S(2)}, u32[]{:S(2)}) async-start(f32[32,1,1345]{2,1,0:T(1,128)} %broadcast_in_dim.8), calls=%async_computation.3 | async-start | bytes 360448 | tf_op jit(solution)/shard_map/all_to_all | solution.py:86
  77.4 11.2 %all-to-all-done.3 = f32[32,1,1345]{2,1,0:T(1,128)S(1)} async-done(((f32[32,1,1345]{2,1,0:T(1,128)}), f32[32,1,1345]{2,1,0:T(1,128)S(1)}, u32[]{:S(2)}, u32[]{:S(2)}) %all-to-all-start.3) | async-done | bytes 172192 | tf_op jit(solution)/shard_map/all_to_all | solution.py:86
  88.6 0.1 reduce_sum.68
  88.7 0.5 slice.32
  89.3 0.7 multiply_reduce_fusion.1
  91.4 0.0 copy-done.6
  91.4 0.0 copy-done.7
  91.4 0.0 copy-done.8
  91.4 0.7 convert_bitcast_fusion
  92.1 16.5 %all-gather.3 = bf16[16,1,3840]{2,1,0:T(2,128)(2,1)S(1)} all-gather(bf16[1,1,3840]{2,1,0:T(2,128)(2,1)S(1)} %get-tuple-element.102), channel_id=1, replica_groups=mesh['z'=8,'y'=8,'c'=2,'tp'=4] {'y','c'}, dimensions={0}, use_global_device_ids=true | all-gather | bytes 130560 | tf_op jit(solution)/shard_map/all_gather | solution.py:109
  108.6 26.5 %all-gather.1 = bf16[128,3840]{1,0:T(8,128)(2,1)S(1)} all-gather(bf16[16,3840]{1,0:T(8,128)(2,1)S(1)} %bitcast.18), channel_id=3, replica_groups=mesh['z'=8,'y'=8,'c'=2,'tp'=4] {'z'}, dimensions={0}, use_global_device_ids=true | all-gather | bytes 1105920 | tf_op jit(solution)/shard_map/all_gather | solution.py:110
  135.1 0.1 fusion.9
  135.2 0.0 copy-start.2
  135.2 0.0 copy-start.3
  135.2 0.0 copy-start.4
  135.3 0.8 reshape.116
  136.1 0.1 reshape.118
  136.2 0.2 reshape.117
  136.4 0.0 copy-start
  136.4 0.1 constant_dynamic-slice_fusion.1
  136.5 0.1 reshape.119
  136.7 0.1 mul.231
  136.8 0.0 copy-done.2
  136.8 0.0 copy-done.3
  136.8 0.8 fusion.5
  137.6 0.1 reshape.120
  137.7 0.1 reshape.134
  137.7 12.5 %all-gather.4 = bf16[4,1,24320]{2,1,0:T(2,128)(2,1)S(1)} all-gather(bf16[1,1,24320]{2,1,0:T(2,128)(2,1)S(1)} %reshape.134), channel_id=4, replica_groups=mesh['z'=8,'y'=8,'c'=2,'tp'=4] {'tp'}, dimensions={0}, use_global_device_ids=true | all-gather | bytes 243200 | tf_op jit(solution)/shard_map/all_gather | solution.py:119
  150.3 0.1 copy.76
  150.4 0.1 slice.38
  150.5 0.0 copy-start.9
  150.5 0.0 copy-start.10
  150.5 0.0 copy-start.11
  150.5 1.0 copy.63
  151.5 0.1 reshape.124
  151.6 0.4 reshape.123
  152.0 0.7 copy.64
  152.8 0.1 reshape.121
  152.9 0.7 reshape.122
  153.6 0.7 constant_dynamic-slice_fusion
  154.3 0.7 multiply_subtract_fusion.2
  (19 shorter events, 0.2 us)
Async XLA Ops:
  0.6 2.1 %copy-start.1 = (bf16[1,192,1280]{2,1,0:T(8,128)(2,1)S(1)}, bf16[1,192,1280]{2,1,0:T(8,128)(2,1)}, u32[]{:S(2)}) copy-start(bf16[1,192,1280]{2,1,0:T(8,128)(2,1)} %param.15) | copy-start | bytes 1474564
  10.7 16.7 %copy-start.12 = (f32[1,1,1344]{2,1,0:T(1,128)S(1)}, f32[1,1,1344]{2,1,0:T(1,128)}, u32[]{:S(2)}) copy-start(f32[1,1,1344]{2,1,0:T(1,128)} %param.16) | copy-start | bytes 16132
  10.7 16.8 %copy-start.5 = (bf16[64,320]{1,0:T(8,128)(2,1)S(1)}, bf16[64,320]{1,0:T(8,128)(2,1)}, u32[]{:S(2)}) copy-start(bf16[64,320]{1,0:T(8,128)(2,1)} %param.17) | copy-start | bytes 122884
  10.7 44.9 %all-to-all-start.1 = ((f32[64,1,3840]{2,1,0:T(1,128)}), f32[64,1,3840]{2,1,0:T(1,128)S(1)}, u32[]{:S(2)}, u32[]{:S(2)}) async-start(f32[64,1,3840]{2,1,0:T(1,128)} %all_to_all.18), calls=%async_computation.1 | async-start | bytes 1966080 | tf_op jit(solution)/shard_map/all_to_all | solution.py:68
  40.6 50.8 %copy-start.6 = (f32[1,3840]{1,0:T(1,128)S(1)}, f32[1,3840]{1,0:T(1,128)}, u32[]{:S(2)}) copy-start(f32[1,3840]{1,0:T(1,128)} %param.18) | copy-start | bytes 46084
  40.6 50.8 %copy-start.7 = (f32[1,3840]{1,0:T(1,128)S(1)}, f32[1,3840]{1,0:T(1,128)}, u32[]{:S(2)}) copy-start(f32[1,3840]{1,0:T(1,128)} %param.20) | copy-start | bytes 46084
  40.6 50.8 %copy-start.8 = (f32[1,3840]{1,0:T(1,128)S(1)}, f32[1,3840]{1,0:T(1,128)}, u32[]{:S(2)}) copy-start(f32[1,3840]{1,0:T(1,128)} %param.19) | copy-start | bytes 46084
  71.2 17.4 %all-to-all-start.3 = ((f32[32,1,1345]{2,1,0:T(1,128)}), f32[32,1,1345]{2,1,0:T(1,128)S(1)}, u32[]{:S(2)}, u32[]{:S(2)}) async-start(f32[32,1,1345]{2,1,0:T(1,128)} %broadcast_in_dim.8), calls=%async_computation.3 | async-start | bytes 360448 | tf_op jit(solution)/shard_map/all_to_all | solution.py:86
  135.2 1.6 %copy-start.2 = (f32[16,1280]{1,0:T(8,128)S(1)}, f32[16,1280]{1,0:T(8,128)}, u32[]{:S(2)}) copy-start(f32[16,1280]{1,0:T(8,128)} %param.21) | copy-start | bytes 245764
  135.2 1.6 %copy-start.3 = (f32[16,1280]{1,0:T(8,128)S(1)}, f32[16,1280]{1,0:T(8,128)}, u32[]{:S(2)}) copy-start(f32[16,1280]{1,0:T(8,128)} %param.23) | copy-start | bytes 245764
  135.2 1.6 %copy-start.4 = (f32[16,1280]{1,0:T(8,128)S(1)}, f32[16,1280]{1,0:T(8,128)}, u32[]{:S(2)}) copy-start(f32[16,1280]{1,0:T(8,128)} %param.22) | copy-start | bytes 245764
  136.4 14.0 %copy-start = (bf16[192,1280]{1,0:T(8,128)(2,1)}, bf16[192,1280]{1,0:T(8,128)(2,1)S(1)}, u32[]{:S(2)}) copy-start(bf16[192,1280]{1,0:T(8,128)(2,1)S(1)} %reshape.117) | copy-start | bytes 1474564
  150.5 3.8 %copy-start.9 = (f32[1344]{0:T(1024)S(1)}, f32[1344]{0:T(1024)}, u32[]{:S(2)}) copy-start(f32[1344]{0:T(1024)} %param.24) | copy-start | bytes 16132
  150.5 3.8 %copy-start.10 = (f32[1344]{0:T(1024)S(1)}, f32[1344]{0:T(1024)}, u32[]{:S(2)}) copy-start(f32[1344]{0:T(1024)} %param.26) | copy-start | bytes 16132
  150.5 3.8 %copy-start.11 = (f32[1344]{0:T(1024)S(1)}, f32[1344]{0:T(1024)}, u32[]{:S(2)}) copy-start(f32[1344]{0:T(1024)} %param.25) | copy-start | bytes 16132

commit v8 on v7

--- a/solution.py
+++ b/solution.py
@@ -116,7 +116,9 @@
     o_block = lax.dynamic_slice_in_dim(o_weight, block_start, block_rows, 1)
     emb_rows = emb_new.astype(jnp.bfloat16)
     payload = jnp.concatenate([q_block.reshape(-1), o_block.reshape(-1), emb_rows.reshape(-1)])
-    shared = lax.all_gather(payload, "tp", axis=0, tiled=False)
+    shared = lax.all_to_all(
+        jnp.broadcast_to(payload[None], (tp_count,) + payload.shape), "tp", 0, 0, tiled=True
+    )
     q_len = block_rows * q_columns
     q_average = (
         shared[:, :q_len]

time: 155 us -> 155 us (level)
  blocking collectives: 84.7 us -> 72.2 us
  waiting for transfers between devices: 26.2 us -> 31.8 us
  starting transfers between devices: 22.2 us -> 25.6 us
  other arithmetic: 6.42 us -> 8.28 us
    all_gather x1 -> x0, blocking collectives: 12.5 us -> none  [body(): shared = lax.all_gather(payload, 'tp', axis=0, tiled=False)]
    all_to_all x0 -> x1, waiting for transfers between devices: none -> 5.55 us  [body(): lax.all_to_all(jnp.broadcast_to(payload[None], (tp_count,) + payload.shap...]
    all_to_all x0 -> x1, starting transfers between devices: none -> 3.36 us  [body(): lax.all_to_all(jnp.broadcast_to(payload[None], (tp_count,) + payload.shap...]
    broadcast_in_dim x0 -> x1, other arithmetic: none -> 1.86 us  [body(): jnp.broadcast_to(payload[None], (tp_count,) + payload.shape)]
    unnamed x32 -> x33, local copies, waits for them, and re-layouts: 3.3 us -> 4.14 us
  transfers between devices with their start and end apart: 2 -> 3, of which waited for: 2 -> 3; matrix products, arithmetic and copies ran while one was open for 0% -> 1% of each run, Pallas kernels for 0% -> 0%
where the time goes in v8:
time: 155 us
  blocking collectives  72.2 us (47%)
  waiting for transfers between devices  31.8 us (21%)
  starting transfers between devices  25.6 us (17%)
  local copies, waits for them, and re-layouts  12.6 us (8%)
  other arithmetic  8.28 us (5%)
  between operations  4.42 us (3%)
    all_gather x1, blocking collectives, body(): gathered = lax.all_gather(gathered, 'z', axis=0, tiled=False).reshape(-1)  26.5 us
    all_to_all x1, starting transfers between devices, body(): pieces = lax.all_to_all(partial, ('z', 'y'), 0, 0, tiled=True)  16.7 us
    all_gather x1, blocking collectives, body(): lax.all_gather(flat_new.astype(jnp.bfloat16), ('y', 'c'), axis=0, tiled=F...  16.5 us
    all_to_all x1, waiting for transfers between devices, body(): pieces = lax.all_to_all(partial, ('z', 'y'), 0, 0, tiled=True)  15 us
    all_gather x1, blocking collectives, body(): emb_blocks = lax.all_gather(emb_grad, 'tp', axis=0, tiled=False)  12.5 us
    all_to_all x1, blocking collectives, body(): packed = jnp.sum(lax.all_to_all(copies, axis, 0, 0, tiled=True), axis=0)  12.1 us
    all_to_all x1, waiting for transfers between devices, body(): packed = jnp.sum(lax.all_to_all(copies, axis, 0, 0, tiled=True), axis=0)  11.2 us
    all_to_all x1, waiting for transfers between devices, body(): lax.all_to_all(jnp.broadcast_to(payload[None], (tp_count,) + payload.shap...  5.55 us
  transfers between devices with their start and end apart: 3, of which 3 were waited for; matrix products, arithmetic and copies ran while one was open for 1% of the time, Pallas kernels for 0%

profile of v8, /device:TPU:8, one launch (start us, length us, event | category | flops | bytes accessed | tf_op | source)
XLA Modules:
  0.0 154.8 jit_solution(18241759480070505873)
XLA Ops:
  0.6 0.0 copy-start.1
  0.7 1.3 copy.57
  2.0 0.7 concatenate.14
  2.7 0.0 copy-done.1
  2.7 0.3 concatenate.15
  3.0 1.3 pad_maximum_fusion
  4.3 0.1 copy.58
  4.4 4.5 %all_to_all.35 = bf16[64,2,3840]{2,0,1:T(8,128)(2,1)S(1)} all-to-all(bf16[64,2,3840]{2,0,1:T(8,128)(2,1)S(1)} %copy.58), channel_id=1, replica_groups=mesh['z'=8,'y'=8,'c'=2,'tp'=4] {'c'}, dimensions={1} | all-to-all | bytes 1966080 | tf_op jit(solution)/shard_map/all_to_all | solution.py:64
  8.9 0.1 convert_reduce_fusion
  9.1 1.6 %all_to_all.24 = f32[64,1,3840]{2,1,0:T(1,128)} reshape(f32[64,3840]{1,0:T(8,128)S(1)} %convert_reduce_fusion) | data formatting | bytes 1966080 | tf_op jit(solution)/shard_map/all_to_all | solution.py:68
  10.7 16.7 %all-to-all-start.1 = ((f32[64,1,3840]{2,1,0:T(1,128)}), f32[64,1,3840]{2,1,0:T(1,128)S(1)}, u32[]{:S(2)}, u32[]{:S(2)}) async-start(f32[64,1,3840]{2,1,0:T(1,128)} %all_to_all.24), calls=%async_computation.1 | async-start | bytes 1966080 | tf_op jit(solution)/shard_map/all_to_all | solution.py:68
  27.4 0.0 copy-done.12
  27.4 0.0 copy-done.5
  27.5 12.5 %all-gather = bf16[256,320]{1,0:T(8,128)(2,1)S(1)} all-gather(bf16[64,320]{1,0:T(8,128)(2,1)S(1)} %copy-done.5), channel_id=2, replica_groups=mesh['z'=8,'y'=8,'c'=2,'tp'=4] {'tp'}, dimensions={0}, use_global_device_ids=true | all-gather | bytes 204800 | tf_op jit(solution)/shard_map/all_gather | solution.py:70
  39.9 0.7 fusion
  40.6 15.0 %all-to-all-done.1 = f32[64,1,3840]{2,1,0:T(1,128)S(1)} async-done(((f32[64,1,3840]{2,1,0:T(1,128)}), f32[64,1,3840]{2,1,0:T(1,128)S(1)}, u32[]{:S(2)}, u32[]{:S(2)}) %all-to-all-start.1) | async-done | bytes 983072 | tf_op jit(solution)/shard_map/all_to_all | solution.py:68
  55.6 0.6 reduce_sum.64
  56.2 0.6 multiply_reduce_fusion
  58.1 0.1 pad_maximum_fusion.2
  58.2 0.1 broadcast_in_dim.9
  58.2 12.1 %all_to_all.36 = f32[16,1,1345]{2,1,0:T(1,128)S(1)} all-to-all(f32[16,1,1345]{2,1,0:T(1,128)S(1)} %broadcast_in_dim.9), channel_id=1, replica_groups=mesh['z'=8,'y'=8,'c'=2,'tp'=4] {'y','c'}, dimensions={0} | all-to-all | bytes 172160 | tf_op jit(solution)/shard_map/all_to_all | solution.py:86
  70.4 0.1 reduce_sum.67
  70.4 0.8 broadcast_in_dim.10
  71.2 5.5 %all-to-all-start.3 = ((f32[32,1,1345]{2,1,0:T(1,128)}), f32[32,1,1345]{2,1,0:T(1,128)S(1)}, u32[]{:S(2)}, u32[]{:S(2)}) async-start(f32[32,1,1345]{2,1,0:T(1,128)} %broadcast_in_dim.10), calls=%async_computation.3 | async-start | bytes 360448 | tf_op jit(solution)/shard_map/all_to_all | solution.py:86
  77.4 11.2 %all-to-all-done.3 = f32[32,1,1345]{2,1,0:T(1,128)S(1)} async-done(((f32[32,1,1345]{2,1,0:T(1,128)}), f32[32,1,1345]{2,1,0:T(1,128)S(1)}, u32[]{:S(2)}, u32[]{:S(2)}) %all-to-all-start.3) | async-done | bytes 172192 | tf_op jit(solution)/shard_map/all_to_all | solution.py:86
  88.6 0.1 reduce_sum.68
  88.7 0.5 slice.32
  89.3 0.7 multiply_reduce_fusion.1
  91.4 0.0 copy-done.6
  91.4 0.0 copy-done.7
  91.4 0.7 convert_bitcast_fusion
  92.1 16.5 %all-gather.2 = bf16[16,1,3840]{2,1,0:T(2,128)(2,1)S(1)} all-gather(bf16[1,1,3840]{2,1,0:T(2,128)(2,1)S(1)} %get-tuple-element.102), channel_id=1, replica_groups=mesh['z'=8,'y'=8,'c'=2,'tp'=4] {'y','c'}, dimensions={0}, use_global_device_ids=true | all-gather | bytes 130560 | tf_op jit(solution)/shard_map/all_gather | solution.py:109
  108.6 26.5 %all-gather.1 = bf16[128,3840]{1,0:T(8,128)(2,1)S(1)} all-gather(bf16[16,3840]{1,0:T(8,128)(2,1)S(1)} %bitcast.18), channel_id=3, replica_groups=mesh['z'=8,'y'=8,'c'=2,'tp'=4] {'z'}, dimensions={0}, use_global_device_ids=true | all-gather | bytes 1105920 | tf_op jit(solution)/shard_map/all_gather | solution.py:110
  135.1 0.1 fusion.9
  135.2 0.8 reshape.122
  136.0 0.0 copy-start.2
  136.0 0.0 copy-start.3
  136.0 0.0 copy-start.4
  136.0 1.0 copy.63
  137.1 0.1 reshape.124
  137.2 0.2 reshape.123
  137.4 0.0 copy-start
  137.4 0.1 constant_dynamic-slice_fusion.1
  137.5 0.1 reshape.125
  137.6 0.1 mul.231
  137.8 0.0 copy-done.2
  137.8 0.8 fusion.5
  138.6 0.1 reshape.126
  138.7 0.2 broadcast_in_dim.11
  138.9 0.5 broadcast.79
  139.4 1.9 %reduce.6 = bf16[4,24320]{1,0:T(4,128)(2,1)S(1)} reduce(bf16[4,1,24320]{2,1,0:T(2,128)(2,1)S(1)} %broadcast_in_dim.11, bf16[]{:T(256)} %broadcast.79), dimensions={1}, to_apply=%broadcast_in_dim.11.reduce_sub_computation | reduce | bytes 389122 | tf_op jit(solution)/shard_map/broadcast_in_dim | solution.py:120
  141.3 0.7 reshape.140
  142.0 3.4 %all-to-all-start.4 = ((bf16[4,2,12160]{2,1,0:T(2,128)(2,1)}), bf16[4,2,12160]{2,1,0:T(2,128)(2,1)S(1)}, u32[]{:S(2)}, u32[]{:S(2)}) async-start(bf16[4,2,12160]{2,1,0:T(2,128)(2,1)} %reshape.140), calls=%async_computation.4 | async-start | bytes 389120 | tf_op jit(solution)/shard_map/all_to_all | solution.py:119
  145.4 0.7 multiply_subtract_fusion.2
  146.1 5.5 %all-to-all-done.4 = bf16[4,2,12160]{2,1,0:T(2,128)(2,1)S(1)} async-done(((bf16[4,2,12160]{2,1,0:T(2,128)(2,1)}), bf16[4,2,12160]{2,1,0:T(2,128)(2,1)S(1)}, u32[]{:S(2)}, u32[]{:S(2)}) %all-to-all-start.4) | async-done | bytes 194592 | tf_op jit(solution)/shard_map/all_to_all | solution.py:119
  151.7 0.1 reshape.141
  151.8 0.1 copy.76
  151.9 0.1 slice.38
  152.0 0.1 reshape.130
  152.1 0.4 reshape.129
  152.5 0.7 copy.64
  153.3 0.1 reshape.127
  153.4 0.7 reshape.128
  154.1 0.7 constant_dynamic-slice_fusion
  (24 shorter events, 0.2 us)
Async XLA Ops:
  0.6 2.1 %copy-start.1 = (bf16[1,192,1280]{2,1,0:T(8,128)(2,1)S(1)}, bf16[1,192,1280]{2,1,0:T(8,128)(2,1)}, u32[]{:S(2)}) copy-start(bf16[1,192,1280]{2,1,0:T(8,128)(2,1)} %param.15) | copy-start | bytes 1474564
  10.7 16.7 %copy-start.12 = (f32[1,1,1344]{2,1,0:T(1,128)S(1)}, f32[1,1,1344]{2,1,0:T(1,128)}, u32[]{:S(2)}) copy-start(f32[1,1,1344]{2,1,0:T(1,128)} %param.16) | copy-start | bytes 16132
  10.7 16.8 %copy-start.5 = (bf16[64,320]{1,0:T(8,128)(2,1)S(1)}, bf16[64,320]{1,0:T(8,128)(2,1)}, u32[]{:S(2)}) copy-start(bf16[64,320]{1,0:T(8,128)(2,1)} %param.17) | copy-start | bytes 122884
  10.7 44.9 %all-to-all-start.1 = ((f32[64,1,3840]{2,1,0:T(1,128)}), f32[64,1,3840]{2,1,0:T(1,128)S(1)}, u32[]{:S(2)}, u32[]{:S(2)}) async-start(f32[64,1,3840]{2,1,0:T(1,128)} %all_to_all.24), calls=%async_computation.1 | async-start | bytes 1966080 | tf_op jit(solution)/shard_map/all_to_all | solution.py:68
  40.6 50.8 %copy-start.6 = (f32[1,3840]{1,0:T(1,128)S(1)}, f32[1,3840]{1,0:T(1,128)}, u32[]{:S(2)}) copy-start(f32[1,3840]{1,0:T(1,128)} %param.18) | copy-start | bytes 46084
  40.6 50.8 %copy-start.7 = (f32[1,3840]{1,0:T(1,128)S(1)}, f32[1,3840]{1,0:T(1,128)}, u32[]{:S(2)}) copy-start(f32[1,3840]{1,0:T(1,128)} %param.20) | copy-start | bytes 46084
  40.6 50.8 %copy-start.8 = (f32[1,3840]{1,0:T(1,128)S(1)}, f32[1,3840]{1,0:T(1,128)}, u32[]{:S(2)}) copy-start(f32[1,3840]{1,0:T(1,128)} %param.19) | copy-start | bytes 46084
  71.2 17.4 %all-to-all-start.3 = ((f32[32,1,1345]{2,1,0:T(1,128)}), f32[32,1,1345]{2,1,0:T(1,128)S(1)}, u32[]{:S(2)}, u32[]{:S(2)}) async-start(f32[32,1,1345]{2,1,0:T(1,128)} %broadcast_in_dim.10), calls=%async_computation.3 | async-start | bytes 360448 | tf_op jit(solution)/shard_map/all_to_all | solution.py:86
  136.0 1.8 %copy-start.2 = (f32[16,1280]{1,0:T(8,128)S(1)}, f32[16,1280]{1,0:T(8,128)}, u32[]{:S(2)}) copy-start(f32[16,1280]{1,0:T(8,128)} %param.21) | copy-start | bytes 245764
  136.0 1.8 %copy-start.3 = (f32[16,1280]{1,0:T(8,128)S(1)}, f32[16,1280]{1,0:T(8,128)}, u32[]{:S(2)}) copy-start(f32[16,1280]{1,0:T(8,128)} %param.23) | copy-start | bytes 245764
  136.0 1.8 %copy-start.4 = (f32[16,1280]{1,0:T(8,128)S(1)}, f32[16,1280]{1,0:T(8,128)}, u32[]{:S(2)}) copy-start(f32[16,1280]{1,0:T(8,128)} %param.22) | copy-start | bytes 245764
  137.4 3.9 %copy-start = (bf16[192,1280]{1,0:T(8,128)(2,1)}, bf16[192,1280]{1,0:T(8,128)(2,1)S(1)}, u32[]{:S(2)}) copy-start(bf16[192,1280]{1,0:T(8,128)(2,1)S(1)} %reshape.123) | copy-start | bytes 1474564
  138.6 6.8 %copy-start.9 = (f32[1344]{0:T(1024)S(1)}, f32[1344]{0:T(1024)}, u32[]{:S(2)}) copy-start(f32[1344]{0:T(1024)} %param.24) | copy-start | bytes 16132
  138.6 6.8 %copy-start.10 = (f32[1344]{0:T(1024)S(1)}, f32[1344]{0:T(1024)}, u32[]{:S(2)}) copy-start(f32[1344]{0:T(1024)} %param.26) | copy-start | bytes 16132
  138.6 6.9 %copy-start.11 = (f32[1344]{0:T(1024)S(1)}, f32[1344]{0:T(1024)}, u32[]{:S(2)}) copy-start(f32[1344]{0:T(1024)} %param.25) | copy-start | bytes 16132
  142.0 9.7 %all-to-all-start.4 = ((bf16[4,2,12160]{2,1,0:T(2,128)(2,1)}), bf16[4,2,12160]{2,1,0:T(2,128)(2,1)S(1)}, u32[]{:S(2)}, u32[]{:S(2)}) async-start(bf16[4,2,12160]{2,1,0:T(2,128)(2,1)} %reshape.140), calls=%async_computation.4 | async-start | bytes 389120 | tf_op jit(solution)/shard_map/all_to_all | solution.py:119

commit v9 on v7

--- a/solution.py
+++ b/solution.py
@@ -80,7 +80,7 @@
     local_squares = jnp.sum(grad_piece * grad_piece) + jnp.sum(emb_piece * emb_piece)
     gains_local = norm_grad[0, 0]
     packed = jnp.concatenate([local_squares[None], gains_local])
-    for axis in (("y", "c"), ("z", "tp")):
+    for axis in (("z", "tp"), ("y", "c")):
         count = lax.axis_size(axis)
         copies = jnp.broadcast_to(packed[None], (count,) + packed.shape)
         packed = jnp.sum(lax.all_to_all(copies, axis, 0, 0, tiled=True), axis=0)

time: 155 us -> 154 us (level)
  blocking collectives: 84.7 us -> 90.8 us
  waiting for transfers between devices: 26.2 us -> 20.9 us
  starting transfers between devices: 22.2 us -> 20.5 us
    all_to_all x1, blocking collectives: 12.1 us -> 18.3 us  [body(): packed = jnp.sum(lax.all_to_all(copies, axis, 0, 0, tiled=True), axis=0)]
    all_to_all x1, waiting for transfers between devices: 11.2 us -> 5.88 us  [body(): packed = jnp.sum(lax.all_to_all(copies, axis, 0, 0, tiled=True), axis=0)]
    all_to_all x1, starting transfers between devices: 5.48 us -> 3.79 us  [body(): packed = jnp.sum(lax.all_to_all(copies, axis, 0, 0, tiled=True), axis=0)]
where the time goes in v9:
time: 154 us
  blocking collectives  90.8 us (59%)
  waiting for transfers between devices  20.9 us (14%)
  starting transfers between devices  20.5 us (13%)
  local copies, waits for them, and re-layouts  11 us (7%)
  other arithmetic  6.42 us (4%)
  between operations  4.38 us (3%)
    all_gather x1, blocking collectives, body(): gathered = lax.all_gather(gathered, 'z', axis=0, tiled=False).reshape(-1)  26.5 us
    all_to_all x1, blocking collectives, body(): packed = jnp.sum(lax.all_to_all(copies, axis, 0, 0, tiled=True), axis=0)  18.3 us
    all_to_all x1, starting transfers between devices, body(): pieces = lax.all_to_all(partial, ('z', 'y'), 0, 0, tiled=True)  16.7 us
    all_gather x1, blocking collectives, body(): lax.all_gather(flat_new.astype(jnp.bfloat16), ('y', 'c'), axis=0, tiled=F...  16.4 us
    all_to_all x1, waiting for transfers between devices, body(): pieces = lax.all_to_all(partial, ('z', 'y'), 0, 0, tiled=True)  15 us
    all_gather x1, blocking collectives, body(): shared = lax.all_gather(payload, 'tp', axis=0, tiled=False)  12.5 us
    all_gather x1, blocking collectives, body(): emb_blocks = lax.all_gather(emb_grad, 'tp', axis=0, tiled=False)  12.5 us
    all_to_all x1, waiting for transfers between devices, body(): packed = jnp.sum(lax.all_to_all(copies, axis, 0, 0, tiled=True), axis=0)  5.88 us
  transfers between devices with their start and end apart: 2, of which 2 were waited for; matrix products, arithmetic and copies ran while one was open for 0% of the time, Pallas kernels for 0%

profile of v9, /device:TPU:8, one launch (start us, length us, event | category | flops | bytes accessed | tf_op | source)
XLA Modules:
  0.0 154.0 jit_solution(5634160040303990888)
XLA Ops:
  0.6 0.0 copy-start.1
  0.7 1.3 copy.57
  2.0 0.7 concatenate.14
  2.7 0.0 copy-done.1
  2.7 0.3 concatenate.15
  3.0 1.3 pad_maximum_fusion
  4.3 0.1 copy.58
  4.4 4.5 %all_to_all.26 = bf16[64,2,3840]{2,0,1:T(8,128)(2,1)S(1)} all-to-all(bf16[64,2,3840]{2,0,1:T(8,128)(2,1)S(1)} %copy.58), channel_id=1, replica_groups=mesh['z'=8,'y'=8,'c'=2,'tp'=4] {'c'}, dimensions={1} | all-to-all | bytes 1966080 | tf_op jit(solution)/shard_map/all_to_all | solution.py:64
  8.9 0.1 convert_reduce_fusion
  9.1 1.6 %all_to_all.18 = f32[64,1,3840]{2,1,0:T(1,128)} reshape(f32[64,3840]{1,0:T(8,128)S(1)} %convert_reduce_fusion) | data formatting | bytes 1966080 | tf_op jit(solution)/shard_map/all_to_all | solution.py:68
  10.7 16.7 %all-to-all-start.1 = ((f32[64,1,3840]{2,1,0:T(1,128)}), f32[64,1,3840]{2,1,0:T(1,128)S(1)}, u32[]{:S(2)}, u32[]{:S(2)}) async-start(f32[64,1,3840]{2,1,0:T(1,128)} %all_to_all.18), calls=%async_computation.1 | async-start | bytes 1966080 | tf_op jit(solution)/shard_map/all_to_all | solution.py:68
  27.4 0.0 copy-done.12
  27.4 0.0 copy-done.5
  27.5 12.5 %all-gather = bf16[256,320]{1,0:T(8,128)(2,1)S(1)} all-gather(bf16[64,320]{1,0:T(8,128)(2,1)S(1)} %copy-done.5), channel_id=2, replica_groups=mesh['z'=8,'y'=8,'c'=2,'tp'=4] {'tp'}, dimensions={0}, use_global_device_ids=true | all-gather | bytes 204800 | tf_op jit(solution)/shard_map/all_gather | solution.py:70
  39.9 0.7 fusion
  40.6 15.0 %all-to-all-done.1 = f32[64,1,3840]{2,1,0:T(1,128)S(1)} async-done(((f32[64,1,3840]{2,1,0:T(1,128)}), f32[64,1,3840]{2,1,0:T(1,128)S(1)}, u32[]{:S(2)}, u32[]{:S(2)}) %all-to-all-start.1) | async-done | bytes 983072 | tf_op jit(solution)/shard_map/all_to_all | solution.py:68
  55.6 0.6 reduce_sum.64
  56.2 0.6 multiply_reduce_fusion
  58.1 0.1 pad_maximum_fusion.2
  58.2 0.1 broadcast_in_dim.7
  58.3 18.3 %all_to_all.27 = f32[32,1,1345]{2,1,0:T(1,128)S(1)} all-to-all(f32[32,1,1345]{2,1,0:T(1,128)S(1)} %broadcast_in_dim.7), channel_id=1, replica_groups=mesh['z'=8,'y'=8,'c'=2,'tp'=4] {'z','tp'}, dimensions={0} | all-to-all | bytes 344320 | tf_op jit(solution)/shard_map/all_to_all | solution.py:86
  76.5 0.1 reduce_sum.67
  76.6 0.7 broadcast_in_dim.8
  77.3 3.8 %all-to-all-start.3 = ((f32[16,1,1345]{2,1,0:T(1,128)}), f32[16,1,1345]{2,1,0:T(1,128)S(1)}, u32[]{:S(2)}, u32[]{:S(2)}) async-start(f32[16,1,1345]{2,1,0:T(1,128)} %broadcast_in_dim.8), calls=%async_computation.3 | async-start | bytes 180224 | tf_op jit(solution)/shard_map/all_to_all | solution.py:86
  81.9 5.9 %all-to-all-done.3 = f32[16,1,1345]{2,1,0:T(1,128)S(1)} async-done(((f32[16,1,1345]{2,1,0:T(1,128)}), f32[16,1,1345]{2,1,0:T(1,128)S(1)}, u32[]{:S(2)}, u32[]{:S(2)}) %all-to-all-start.3) | async-done | bytes 86112 | tf_op jit(solution)/shard_map/all_to_all | solution.py:86
  87.7 0.1 reduce_sum.68
  87.8 0.5 slice.32
  88.3 0.7 multiply_reduce_fusion.1
  90.4 0.0 copy-done.6
  90.4 0.0 copy-done.7
  90.4 0.0 copy-done.8
  90.4 0.7 convert_bitcast_fusion
  91.2 16.4 %all-gather.3 = bf16[16,1,3840]{2,1,0:T(2,128)(2,1)S(1)} all-gather(bf16[1,1,3840]{2,1,0:T(2,128)(2,1)S(1)} %get-tuple-element.102), channel_id=1, replica_groups=mesh['z'=8,'y'=8,'c'=2,'tp'=4] {'y','c'}, dimensions={0}, use_global_device_ids=true | all-gather | bytes 130560 | tf_op jit(solution)/shard_map/all_gather | solution.py:109
  107.6 26.5 %all-gather.1 = bf16[128,3840]{1,0:T(8,128)(2,1)S(1)} all-gather(bf16[16,3840]{1,0:T(8,128)(2,1)S(1)} %bitcast.18), channel_id=3, replica_groups=mesh['z'=8,'y'=8,'c'=2,'tp'=4] {'z'}, dimensions={0}, use_global_device_ids=true | all-gather | bytes 1105920 | tf_op jit(solution)/shard_map/all_gather | solution.py:110
  134.2 0.1 fusion.9
  134.2 0.0 copy-start.2
  134.2 0.0 copy-start.3
  134.2 0.0 copy-start.4
  134.3 0.8 reshape.116
  135.1 0.1 reshape.118
  135.2 0.2 reshape.117
  135.4 0.0 copy-start
  135.4 0.1 constant_dynamic-slice_fusion.1
  135.5 0.1 reshape.119
  135.7 0.1 mul.231
  135.8 0.0 copy-done.3
  135.8 0.0 copy-done.4
  135.8 0.8 fusion.5
  136.6 0.1 reshape.120
  136.7 0.1 reshape.134
  136.7 12.5 %all-gather.4 = bf16[4,1,24320]{2,1,0:T(2,128)(2,1)S(1)} all-gather(bf16[1,1,24320]{2,1,0:T(2,128)(2,1)S(1)} %reshape.134), channel_id=4, replica_groups=mesh['z'=8,'y'=8,'c'=2,'tp'=4] {'tp'}, dimensions={0}, use_global_device_ids=true | all-gather | bytes 243200 | tf_op jit(solution)/shard_map/all_gather | solution.py:119
  149.3 0.1 copy.76
  149.4 0.1 slice.38
  149.5 0.0 copy-start.9
  149.5 0.0 copy-start.10
  149.5 0.0 copy-start.11
  149.5 1.0 copy.63
  150.5 0.1 reshape.124
  150.6 0.4 reshape.123
  151.0 0.7 copy.64
  151.8 0.1 reshape.121
  151.9 0.7 reshape.122
  152.6 0.7 constant_dynamic-slice_fusion
  153.3 0.7 multiply_subtract_fusion.2
  (19 shorter events, 0.2 us)
Async XLA Ops:
  0.6 2.1 %copy-start.1 = (bf16[1,192,1280]{2,1,0:T(8,128)(2,1)S(1)}, bf16[1,192,1280]{2,1,0:T(8,128)(2,1)}, u32[]{:S(2)}) copy-start(bf16[1,192,1280]{2,1,0:T(8,128)(2,1)} %param.15) | copy-start | bytes 1474564
  10.7 16.7 %copy-start.12 = (f32[1,1,1344]{2,1,0:T(1,128)S(1)}, f32[1,1,1344]{2,1,0:T(1,128)}, u32[]{:S(2)}) copy-start(f32[1,1,1344]{2,1,0:T(1,128)} %param.16) | copy-start | bytes 16132
  10.7 16.8 %copy-start.5 = (bf16[64,320]{1,0:T(8,128)(2,1)S(1)}, bf16[64,320]{1,0:T(8,128)(2,1)}, u32[]{:S(2)}) copy-start(bf16[64,320]{1,0:T(8,128)(2,1)} %param.17) | copy-start | bytes 122884
  10.7 44.9 %all-to-all-start.1 = ((f32[64,1,3840]{2,1,0:T(1,128)}), f32[64,1,3840]{2,1,0:T(1,128)S(1)}, u32[]{:S(2)}, u32[]{:S(2)}) async-start(f32[64,1,3840]{2,1,0:T(1,128)} %all_to_all.18), calls=%async_computation.1 | async-start | bytes 1966080 | tf_op jit(solution)/shard_map/all_to_all | solution.py:68
  40.6 49.8 %copy-start.6 = (f32[1,3840]{1,0:T(1,128)S(1)}, f32[1,3840]{1,0:T(1,128)}, u32[]{:S(2)}) copy-start(f32[1,3840]{1,0:T(1,128)} %param.18) | copy-start | bytes 46084
  40.6 49.8 %copy-start.7 = (f32[1,3840]{1,0:T(1,128)S(1)}, f32[1,3840]{1,0:T(1,128)}, u32[]{:S(2)}) copy-start(f32[1,3840]{1,0:T(1,128)} %param.20) | copy-start | bytes 46084
  40.6 49.8 %copy-start.8 = (f32[1,3840]{1,0:T(1,128)S(1)}, f32[1,3840]{1,0:T(1,128)}, u32[]{:S(2)}) copy-start(f32[1,3840]{1,0:T(1,128)} %param.19) | copy-start | bytes 46084
  77.3 10.4 %all-to-all-start.3 = ((f32[16,1,1345]{2,1,0:T(1,128)}), f32[16,1,1345]{2,1,0:T(1,128)S(1)}, u32[]{:S(2)}, u32[]{:S(2)}) async-start(f32[16,1,1345]{2,1,0:T(1,128)} %broadcast_in_dim.8), calls=%async_computation.3 | async-start | bytes 180224 | tf_op jit(solution)/shard_map/all_to_all | solution.py:86
  134.2 1.6 %copy-start.2 = (f32[16,1280]{1,0:T(8,128)S(1)}, f32[16,1280]{1,0:T(8,128)}, u32[]{:S(2)}) copy-start(f32[16,1280]{1,0:T(8,128)} %param.21) | copy-start | bytes 245764
  134.2 1.6 %copy-start.3 = (f32[16,1280]{1,0:T(8,128)S(1)}, f32[16,1280]{1,0:T(8,128)}, u32[]{:S(2)}) copy-start(f32[16,1280]{1,0:T(8,128)} %param.23) | copy-start | bytes 245764
  134.2 1.6 %copy-start.4 = (f32[16,1280]{1,0:T(8,128)S(1)}, f32[16,1280]{1,0:T(8,128)}, u32[]{:S(2)}) copy-start(f32[16,1280]{1,0:T(8,128)} %param.22) | copy-start | bytes 245764
  135.4 14.0 %copy-start = (bf16[192,1280]{1,0:T(8,128)(2,1)}, bf16[192,1280]{1,0:T(8,128)(2,1)S(1)}, u32[]{:S(2)}) copy-start(bf16[192,1280]{1,0:T(8,128)(2,1)S(1)} %reshape.117) | copy-start | bytes 1474564
  149.5 3.8 %copy-start.9 = (f32[1344]{0:T(1024)S(1)}, f32[1344]{0:T(1024)}, u32[]{:S(2)}) copy-start(f32[1344]{0:T(1024)} %param.24) | copy-start | bytes 16132
  149.5 3.8 %copy-start.10 = (f32[1344]{0:T(1024)S(1)}, f32[1344]{0:T(1024)}, u32[]{:S(2)}) copy-start(f32[1344]{0:T(1024)} %param.26) | copy-start | bytes 16132
  149.5 3.8 %copy-start.11 = (f32[1344]{0:T(1024)S(1)}, f32[1344]{0:T(1024)}, u32[]{:S(2)}) copy-start(f32[1344]{0:T(1024)} %param.25) | copy-start | bytes 16132

commit v10 on v9

--- a/solution.py
+++ b/solution.py
@@ -115,7 +115,7 @@
     q_block = lax.dynamic_slice_in_dim(q_weight, block_start, block_rows, 0)
     o_block = lax.dynamic_slice_in_dim(o_weight, block_start, block_rows, 1)
     emb_rows = emb_new.astype(jnp.bfloat16)
-    payload = jnp.concatenate([q_block.reshape(-1), o_block.reshape(-1), emb_rows.reshape(-1)])
+    payload = jnp.concatenate([q_block.reshape(-1), o_block.T.reshape(-1), emb_rows.reshape(-1)])
     shared = lax.all_gather(payload, "tp", axis=0, tiled=False)
     q_len = block_rows * q_columns
     q_average = (
@@ -124,7 +124,13 @@
         .transpose(1, 0, 2)
         .reshape(block_rows, tp_count * q_columns)
     )
-    o_average = shared[:, q_len : 2 * q_len].reshape(tp_count * q_columns, block_rows)
+    o_average = (
+        shared[:, q_len : 2 * q_len]
+        .reshape(tp_count, block_rows, q_columns)
+        .transpose(1, 0, 2)
+        .reshape(block_rows, tp_count * q_columns)
+        .T
+    )
     emb_all = shared[:, 2 * q_len :].reshape(tp_count * emb_new.shape[0], width)
     emb_cols = width // tp_count
     emb_weight = lax.dynamic_slice_in_dim(emb_all, lax.axis_index("tp") * emb_cols, emb_cols, 1)

time: 154 us -> 154 us (level)
    unnamed x32 -> x31, local copies, waits for them, and re-layouts: 3.3 us -> 2.56 us
where the time goes in v10:
time: 154 us
  blocking collectives  90.8 us (59%)
  waiting for transfers between devices  20.9 us (14%)
  starting transfers between devices  20.5 us (13%)
  local copies, waits for them, and re-layouts  10.8 us (7%)
  other arithmetic  6.42 us (4%)
  between operations  4.38 us (3%)
    all_gather x1, blocking collectives, body(): gathered = lax.all_gather(gathered, 'z', axis=0, tiled=False).reshape(-1)  26.5 us
    all_to_all x1, blocking collectives, body(): packed = jnp.sum(lax.all_to_all(copies, axis, 0, 0, tiled=True), axis=0)  18.3 us
    all_to_all x1, starting transfers between devices, body(): pieces = lax.all_to_all(partial, ('z', 'y'), 0, 0, tiled=True)  16.7 us
    all_gather x1, blocking collectives, body(): lax.all_gather(flat_new.astype(jnp.bfloat16), ('y', 'c'), axis=0, tiled=F...  16.4 us
    all_to_all x1, waiting for transfers between devices, body(): pieces = lax.all_to_all(partial, ('z', 'y'), 0, 0, tiled=True)  15 us
    all_gather x1, blocking collectives, body(): shared = lax.all_gather(payload, 'tp', axis=0, tiled=False)  12.5 us
    all_gather x1, blocking collectives, body(): emb_blocks = lax.all_gather(emb_grad, 'tp', axis=0, tiled=False)  12.5 us
    all_to_all x1, waiting for transfers between devices, body(): packed = jnp.sum(lax.all_to_all(copies, axis, 0, 0, tiled=True), axis=0)  5.88 us
  transfers between devices with their start and end apart: 2, of which 2 were waited for; matrix products, arithmetic and copies ran while one was open for 0% of the time, Pallas kernels for 0%

profile of v10, /device:TPU:8, one launch (start us, length us, event | category | flops | bytes accessed | tf_op | source)
XLA Modules:
  0.0 153.7 jit_solution(9290437433854289468)
XLA Ops:
  0.6 0.0 copy-start.1
  0.7 1.3 copy.62
  2.0 0.7 concatenate.14
  2.7 0.0 copy-done.1
  2.7 0.3 concatenate.15
  3.0 1.3 pad_maximum_fusion
  4.3 0.1 copy.63
  4.4 4.5 %all_to_all.26 = bf16[64,2,3840]{2,0,1:T(8,128)(2,1)S(1)} all-to-all(bf16[64,2,3840]{2,0,1:T(8,128)(2,1)S(1)} %copy.63), channel_id=1, replica_groups=mesh['z'=8,'y'=8,'c'=2,'tp'=4] {'c'}, dimensions={1} | all-to-all | bytes 1966080 | tf_op jit(solution)/shard_map/all_to_all | solution.py:64
  8.9 0.1 convert_reduce_fusion
  9.1 1.6 %all_to_all.18 = f32[64,1,3840]{2,1,0:T(1,128)} reshape(f32[64,3840]{1,0:T(8,128)S(1)} %convert_reduce_fusion) | data formatting | bytes 1966080 | tf_op jit(solution)/shard_map/all_to_all | solution.py:68
  10.7 16.7 %all-to-all-start.1 = ((f32[64,1,3840]{2,1,0:T(1,128)}), f32[64,1,3840]{2,1,0:T(1,128)S(1)}, u32[]{:S(2)}, u32[]{:S(2)}) async-start(f32[64,1,3840]{2,1,0:T(1,128)} %all_to_all.18), calls=%async_computation.1 | async-start | bytes 1966080 | tf_op jit(solution)/shard_map/all_to_all | solution.py:68
  27.4 0.0 copy-done.12
  27.5 12.5 %all-gather = bf16[256,320]{1,0:T(8,128)(2,1)S(1)} all-gather(bf16[64,320]{1,0:T(8,128)(2,1)S(1)} %copy-done.5), channel_id=2, replica_groups=mesh['z'=8,'y'=8,'c'=2,'tp'=4] {'tp'}, dimensions={0}, use_global_device_ids=true | all-gather | bytes 204800 | tf_op jit(solution)/shard_map/all_gather | solution.py:70
  39.9 0.7 fusion
  40.6 15.0 %all-to-all-done.1 = f32[64,1,3840]{2,1,0:T(1,128)S(1)} async-done(((f32[64,1,3840]{2,1,0:T(1,128)}), f32[64,1,3840]{2,1,0:T(1,128)S(1)}, u32[]{:S(2)}, u32[]{:S(2)}) %all-to-all-start.1) | async-done | bytes 983072 | tf_op jit(solution)/shard_map/all_to_all | solution.py:68
  55.6 0.6 reduce_sum.64
  56.2 0.6 multiply_reduce_fusion
  58.1 0.1 pad_maximum_fusion.2
  58.2 0.1 broadcast_in_dim.7
  58.3 18.3 %all_to_all.27 = f32[32,1,1345]{2,1,0:T(1,128)S(1)} all-to-all(f32[32,1,1345]{2,1,0:T(1,128)S(1)} %broadcast_in_dim.7), channel_id=1, replica_groups=mesh['z'=8,'y'=8,'c'=2,'tp'=4] {'z','tp'}, dimensions={0} | all-to-all | bytes 344320 | tf_op jit(solution)/shard_map/all_to_all | solution.py:86
  76.5 0.1 reduce_sum.67
  76.6 0.7 broadcast_in_dim.8
  77.3 3.8 %all-to-all-start.3 = ((f32[16,1,1345]{2,1,0:T(1,128)}), f32[16,1,1345]{2,1,0:T(1,128)S(1)}, u32[]{:S(2)}, u32[]{:S(2)}) async-start(f32[16,1,1345]{2,1,0:T(1,128)} %broadcast_in_dim.8), calls=%async_computation.3 | async-start | bytes 180224 | tf_op jit(solution)/shard_map/all_to_all | solution.py:86
  81.9 5.9 %all-to-all-done.3 = f32[16,1,1345]{2,1,0:T(1,128)S(1)} async-done(((f32[16,1,1345]{2,1,0:T(1,128)}), f32[16,1,1345]{2,1,0:T(1,128)S(1)}, u32[]{:S(2)}, u32[]{:S(2)}) %all-to-all-start.3) | async-done | bytes 86112 | tf_op jit(solution)/shard_map/all_to_all | solution.py:86
  87.7 0.1 reduce_sum.68
  87.8 0.5 slice.32
  88.3 0.7 multiply_reduce_fusion.1
  90.4 0.0 copy-done.6
  90.4 0.0 copy-done.7
  90.4 0.0 copy-done.8
  90.4 0.7 convert_bitcast_fusion
  91.2 16.4 %all-gather.3 = bf16[16,1,3840]{2,1,0:T(2,128)(2,1)S(1)} all-gather(bf16[1,1,3840]{2,1,0:T(2,128)(2,1)S(1)} %get-tuple-element.102), channel_id=1, replica_groups=mesh['z'=8,'y'=8,'c'=2,'tp'=4] {'y','c'}, dimensions={0}, use_global_device_ids=true | all-gather | bytes 130560 | tf_op jit(solution)/shard_map/all_gather | solution.py:109
  107.6 26.5 %all-gather.1 = bf16[128,3840]{1,0:T(8,128)(2,1)S(1)} all-gather(bf16[16,3840]{1,0:T(8,128)(2,1)S(1)} %bitcast.22), channel_id=3, replica_groups=mesh['z'=8,'y'=8,'c'=2,'tp'=4] {'z'}, dimensions={0}, use_global_device_ids=true | all-gather | bytes 1105920 | tf_op jit(solution)/shard_map/all_gather | solution.py:110
  134.2 0.1 fusion.9
  134.2 0.0 copy-start.2
  134.2 0.0 copy-start.3
  134.2 0.0 copy-start.4
  134.3 0.8 reshape.119
  135.1 0.1 reshape.121
  135.2 0.2 reshape.120
  135.4 0.0 copy-start
  135.4 0.1 dynamic-slice_bitcast_fusion
  135.5 0.1 copy.67
  135.6 0.1 reshape.122
  135.7 0.1 mul.231
  135.8 0.8 fusion.5
  136.6 0.1 reshape.123
  136.7 0.1 reshape.138
  136.8 12.5 %all-gather.4 = bf16[4,1,24320]{2,1,0:T(2,128)(2,1)S(1)} all-gather(bf16[1,1,24320]{2,1,0:T(2,128)(2,1)S(1)} %reshape.138), channel_id=4, replica_groups=mesh['z'=8,'y'=8,'c'=2,'tp'=4] {'tp'}, dimensions={0}, use_global_device_ids=true | all-gather | bytes 243200 | tf_op jit(solution)/shard_map/all_gather | solution.py:119
  149.3 0.1 copy.82
  149.4 0.1 slice.38
  149.5 0.0 copy-start.9
  149.5 0.0 copy-start.10
  149.5 0.0 copy-start.11
  149.5 1.0 copy.70
  150.5 0.1 reshape.128
  150.6 0.1 reshape.126
  150.8 0.7 reshape.127
  151.5 0.1 reshape.124
  151.6 0.7 reshape.125
  152.3 0.7 constant_dynamic-slice_fusion
  153.0 0.0 copy-done.9
  153.0 0.0 copy-done.11
  153.0 0.7 multiply_subtract_fusion.2
  (21 shorter events, 0.2 us)
Async XLA Ops:
  0.6 2.1 %copy-start.1 = (bf16[1,192,1280]{2,1,0:T(8,128)(2,1)S(1)}, bf16[1,192,1280]{2,1,0:T(8,128)(2,1)}, u32[]{:S(2)}) copy-start(bf16[1,192,1280]{2,1,0:T(8,128)(2,1)} %param.15) | copy-start | bytes 1474564
  10.7 16.7 %copy-start.12 = (f32[1,1,1344]{2,1,0:T(1,128)S(1)}, f32[1,1,1344]{2,1,0:T(1,128)}, u32[]{:S(2)}) copy-start(f32[1,1,1344]{2,1,0:T(1,128)} %param.16) | copy-start | bytes 16132
  10.7 16.8 %copy-start.5 = (bf16[64,320]{1,0:T(8,128)(2,1)S(1)}, bf16[64,320]{1,0:T(8,128)(2,1)}, u32[]{:S(2)}) copy-start(bf16[64,320]{1,0:T(8,128)(2,1)} %param.17) | copy-start | bytes 122884
  10.7 44.9 %all-to-all-start.1 = ((f32[64,1,3840]{2,1,0:T(1,128)}), f32[64,1,3840]{2,1,0:T(1,128)S(1)}, u32[]{:S(2)}, u32[]{:S(2)}) async-start(f32[64,1,3840]{2,1,0:T(1,128)} %all_to_all.18), calls=%async_computation.1 | async-start | bytes 1966080 | tf_op jit(solution)/shard_map/all_to_all | solution.py:68
  40.6 49.8 %copy-start.6 = (f32[1,3840]{1,0:T(1,128)S(1)}, f32[1,3840]{1,0:T(1,128)}, u32[]{:S(2)}) copy-start(f32[1,3840]{1,0:T(1,128)} %param.18) | copy-start | bytes 46084
  40.6 49.8 %copy-start.7 = (f32[1,3840]{1,0:T(1,128)S(1)}, f32[1,3840]{1,0:T(1,128)}, u32[]{:S(2)}) copy-start(f32[1,3840]{1,0:T(1,128)} %param.20) | copy-start | bytes 46084
  40.6 49.8 %copy-start.8 = (f32[1,3840]{1,0:T(1,128)S(1)}, f32[1,3840]{1,0:T(1,128)}, u32[]{:S(2)}) copy-start(f32[1,3840]{1,0:T(1,128)} %param.19) | copy-start | bytes 46084
  77.3 10.4 %all-to-all-start.3 = ((f32[16,1,1345]{2,1,0:T(1,128)}), f32[16,1,1345]{2,1,0:T(1,128)S(1)}, u32[]{:S(2)}, u32[]{:S(2)}) async-start(f32[16,1,1345]{2,1,0:T(1,128)} %broadcast_in_dim.8), calls=%async_computation.3 | async-start | bytes 180224 | tf_op jit(solution)/shard_map/all_to_all | solution.py:86
  134.2 1.6 %copy-start.2 = (f32[16,1280]{1,0:T(8,128)S(1)}, f32[16,1280]{1,0:T(8,128)}, u32[]{:S(2)}) copy-start(f32[16,1280]{1,0:T(8,128)} %param.21) | copy-start | bytes 245764
  134.2 1.6 %copy-start.3 = (f32[16,1280]{1,0:T(8,128)S(1)}, f32[16,1280]{1,0:T(8,128)}, u32[]{:S(2)}) copy-start(f32[16,1280]{1,0:T(8,128)} %param.23) | copy-start | bytes 245764
  134.2 1.6 %copy-start.4 = (f32[16,1280]{1,0:T(8,128)S(1)}, f32[16,1280]{1,0:T(8,128)}, u32[]{:S(2)}) copy-start(f32[16,1280]{1,0:T(8,128)} %param.22) | copy-start | bytes 245764
  135.4 14.0 %copy-start = (bf16[192,1280]{1,0:T(8,128)(2,1)}, bf16[192,1280]{1,0:T(8,128)(2,1)S(1)}, u32[]{:S(2)}) copy-start(bf16[192,1280]{1,0:T(8,128)(2,1)S(1)} %reshape.120) | copy-start | bytes 1474564
  149.5 3.5 %copy-start.9 = (f32[1344]{0:T(1024)S(1)}, f32[1344]{0:T(1024)}, u32[]{:S(2)}) copy-start(f32[1344]{0:T(1024)} %param.24) | copy-start | bytes 16132
  149.5 3.5 %copy-start.10 = (f32[1344]{0:T(1024)S(1)}, f32[1344]{0:T(1024)}, u32[]{:S(2)}) copy-start(f32[1344]{0:T(1024)} %param.26) | copy-start | bytes 16132
  149.5 3.5 %copy-start.11 = (f32[1344]{0:T(1024)S(1)}, f32[1344]{0:T(1024)}, u32[]{:S(2)}) copy-start(f32[1344]{0:T(1024)} %param.25) | copy-start | bytes 16132
